TPU v7x, 256 devices: a whole 4x4x8 slice. The times are simulated.
256 devices in a mesh: date: 2 (over z_hi), strip: 128 (over z_lo, y, x, core).
Axes of the slice: x: 4, y: 4, z: 8 (z_hi: 2, z_lo: 4; z = z_hi * 4 + z_lo), core: 2. Of those that a mesh axis runs over, the one named last changes fastest.
Arguments:
- raw_echoes: bfloat16 [2, 4, 8192, 1024], P(None, 'date', 'strip'), may hold values from -6 to 6
- range_phase: float32 [1024], replicated, may hold values from -3.140625 to 3.140625
- azimuth_phase: float32 [8192], replicated, may hold values from -3.140625 to 3.140625
- calibration: float32 [4, 1024], P(None, ('date', 'strip')), may hold values from 1 to 10
Outputs:
- linked: float32 [2, 4, 1024, 8192], P(None, None, ('date', 'strip'))
- quality: float32 [1024, 8192], P(('date', 'strip'))
All inputs are finite; a program needn't handle non-finite values.
Results may differ from a plain program's by a relative error of at most 0.0003.
Values may be sent and summed in bfloat16 or wider, within the bound.
No kernel may reach another device: no remote copies, remote signals or barrier semaphores. Data moves between devices by JAX's collectives and lax.ppermute only.
A program may use at most 64 MiB of HBM per device.

v0:
```python
import math

import jax
import jax.numpy as jnp
from jax import lax
from jax.experimental import pallas as pl
from jax.experimental.pallas import tpu as pltpu
from jax.sharding import PartitionSpec as P

WIN_HALF = 11
POWER_ITERS = 6
SMOOTH_PASSES = 2


HIGHEST = lax.Precision.HIGHEST
BLOCK = 512
EDGE = 128
CHUNK = 128


def window_lines(values):
    ones = values + pltpu.roll(values, 1, 1)
    twos = ones + pltpu.roll(ones, 2, 1)
    fours = twos + pltpu.roll(twos, 4, 1)
    eights = fours + pltpu.roll(fours, 8, 1)
    width = values.shape[1]
    return (
        pltpu.roll(eights, width - WIN_HALF, 1)
        + pltpu.roll(twos, 5, 1)
        + pltpu.roll(ones, 9, 1)
        + pltpu.roll(values, WIN_HALF, 1)
    )


def link_kernel(mask_ref, prev_ref, cur_ref, next_ref, vec_ref, qual_ref, image, sums):
    step = pl.program_id(0)
    last = pl.num_programs(0) - 1
    dates = cur_ref.shape[1]
    block = cur_ref.shape[3]
    image[:, :, :, EDGE : EDGE + block] = cur_ref[...]
    image[:, :, :, :EDGE] = jnp.where(step > 0, prev_ref[...], 0.0)
    image[:, :, :, EDGE + block :] = jnp.where(step < last, next_ref[...], 0.0)
    rows = sums.shape[1]
    pairs = [(a, b) for a in range(dates) for b in range(a + 1, dates)]

    def part(p, d, shift):
        return image[p, d, pl.ds(shift, rows), :]

    def term(kind, a, b, shift):
        ra, ia = part(0, a, shift), part(1, a, shift)
        if kind == 0:
            return ra * ra + ia * ia
        rb, ib = part(0, b, shift), part(1, b, shift)
        if kind == 1:
            return ra * rb + ia * ib
        return ia * rb - ra * ib

    specs = [(0, a, a) for a in range(dates)]
    for a, b in pairs:
        specs.append((1, a, b))
        specs.append((2, a, b))
    for number, (kind, a, b) in enumerate(specs):
        across = term(kind, a, b, 0) + term(kind, a, b, 1) + term(kind, a, b, 2)
        total = window_lines(across)
        sums[number] = total[:, EDGE : EDGE + block]

    mask = mask_ref[...]
    scale = 3 * (2 * WIN_HALF + 1)

    def chunk_body(index, carry):
        start = pl.multiple_of(index * CHUNK, CHUNK)
        window = [sums[number, :, pl.ds(start, CHUNK)] / scale for number in range(len(specs))]
        powers = [window[a] + 1e-06 for a in range(dates)]
        coherence = {}
        for number, (a, b) in enumerate(pairs):
            factor = lax.rsqrt(powers[a] * powers[b])
            coherence[a, b] = (
                window[dates + 2 * number] * factor,
                window[dates + 2 * number + 1] * factor,
            )
        vector_real = [jnp.ones_like(powers[0]) for _ in range(dates)]
        vector_imag = [jnp.zeros_like(powers[0]) for _ in range(dates)]
        for iteration in range(POWER_ITERS):
            new_real = []
            new_imag = []
            for target in range(dates):
                acc_real = vector_real[target]
                acc_imag = vector_imag[target]
                for source in range(dates):
                    if source != target:
                        if target < source:
                            part_real, part_imag = coherence[target, source]
                        else:
                            part_real, part_imag = coherence[source, target]
                            part_imag = -part_imag
                        acc_real = (
                            acc_real + part_real * vector_real[source] - part_imag * vector_imag[source]
                        )
                        acc_imag = (
                            acc_imag + part_real * vector_imag[source] + part_imag * vector_real[source]
                        )
                new_real.append(acc_real)
                new_imag.append(acc_imag)
            mean_square = (
                sum(new_real[t] * new_real[t] + new_imag[t] * new_imag[t] for t in range(dates)) / dates
            )
            factor = lax.rsqrt(jnp.maximum(mean_square, 1.0))
            vector_real = [entry * factor for entry in new_real]
            vector_imag = [entry * factor for entry in new_imag]
        magnitude = sum(
            jnp.sqrt(coherence[pair][0] * coherence[pair][0] + coherence[pair][1] * coherence[pair][1])
            for pair in pairs
        ) / len(pairs)
        quality = mask * (0.05 + magnitude)
        vectors = vector_real + vector_imag
        for passes in range(SMOOTH_PASSES):
            denominator = quality + pltpu.roll(quality, 1, 0) + pltpu.roll(quality, rows - 1, 0)
            denominator = jnp.where(denominator > 0, denominator, 1.0)
            smoothed = []
            for entry in vectors:
                weighted = entry * quality
                numerator = weighted + pltpu.roll(weighted, 1, 0) + pltpu.roll(weighted, rows - 1, 0)
                smoothed.append(numerator / denominator)
            vectors = smoothed
        keep = slice(SMOOTH_PASSES, rows - SMOOTH_PASSES)
        for number, entry in enumerate(vectors):
            vec_ref[number // dates, number % dates, :, pl.ds(start, CHUNK)] = entry[keep]
        qual_ref[:, pl.ds(start, CHUNK)] = quality[keep]
        return carry

    lax.fori_loop(0, block // CHUNK, chunk_body, 0)


def link_and_smooth(extended, valid_mask):
    parts, dates, columns, lines = extended.shape
    rows = columns - 2
    kept = rows - 2 * SMOOTH_PASSES
    steps = lines // BLOCK
    per_block = BLOCK // EDGE
    edges = lines // EDGE
    mask = jnp.broadcast_to(valid_mask[:, None], (rows, CHUNK))
    return pl.pallas_call(
        link_kernel,
        grid=(steps,),
        in_specs=[
            pl.BlockSpec((rows, CHUNK), lambda i: (0, 0)),
            pl.BlockSpec((parts, dates, columns, EDGE), lambda i: (0, 0, 0, jnp.maximum(i * per_block - 1, 0))),
            pl.BlockSpec((parts, dates, columns, BLOCK), lambda i: (0, 0, 0, i)),
            pl.BlockSpec((parts, dates, columns, EDGE), lambda i: (0, 0, 0, jnp.minimum((i + 1) * per_block, edges - 1))),
        ],
        out_specs=[
            pl.BlockSpec((parts, dates, kept, BLOCK), lambda i: (0, 0, 0, i)),
            pl.BlockSpec((kept, BLOCK), lambda i: (0, i)),
        ],
        out_shape=[
            jax.ShapeDtypeStruct((parts, dates, kept, lines), jnp.float32),
            jax.ShapeDtypeStruct((kept, lines), jnp.float32),
        ],
        scratch_shapes=[
            pltpu.VMEM((parts, dates, columns, BLOCK + 2 * EDGE), jnp.float32),
            pltpu.VMEM((dates + dates * (dates - 1), rows, BLOCK), jnp.float32),
        ],
    )(mask, extended, extended, extended)


def split_up(x, dim, count):
    shape = x.shape
    tiles = x.reshape(*shape[:dim], count, shape[dim] // count, *shape[dim + 1 :])
    return jnp.moveaxis(tiles, dim, 0)


def laid_out(tiles, dim):
    shape = list(tiles.shape[1:])
    shape[dim] *= tiles.shape[0]
    return jnp.moveaxis(tiles, 0, dim).reshape(shape)


def one_exchange(x, axis, axes, splits, concats):
    sizes = [lax.axis_size(a) for a in axes]
    tiles = split_up(x, splits[0], sizes[0])
    tiles = jnp.moveaxis(split_up(tiles, splits[1] + 1, sizes[1]), 0, 1)
    inside = tiles.shape[2:]
    tiles = tiles.reshape(-1, *inside)
    tiles = lax.all_to_all(tiles, axis, split_axis=0, concat_axis=0, tiled=True)
    tiles = laid_out(tiles.reshape(*sizes, *inside), concats[0] + 1)
    return laid_out(tiles, concats[1])


def extended_2(x, sides, width):
    edges = {}
    for axis, dim in sides:
        count, length = (lax.axis_size(axis), x.shape[dim])
        up = [(i, (i + 1) % count) for i in range(count - 1)]
        last = lax.slice_in_dim(x, length - width, length, axis=dim)
        first = lax.slice_in_dim(x, 0, width, axis=dim)
        edges[dim] = (
            lax.ppermute(last, axis, up),
            lax.ppermute(first, axis, [(b, a) for a, b in up]),
        )
    done = []
    for _, dim in sides:
        low, high = edges[dim]
        around = [(width, width) if d in done else (0, 0) for d in range(x.ndim)]
        x = jnp.concatenate([jnp.pad(low, around), x, jnp.pad(high, around)], axis=dim)
        done.append(dim)
    return x


def dft_table(length, direction):
    counter = jnp.arange(length, dtype=jnp.int32)
    product = counter[:, None] * counter[None, :] % length
    angles = product.astype(jnp.float32) * (direction * 2.0 * math.pi / length)
    cosine = jnp.cos(angles)
    sine_part = jnp.sin(angles)
    return jnp.stack([jnp.stack([cosine, -sine_part]), jnp.stack([sine_part, cosine])])


def twiddle(outer_size, inner_size, direction):
    product = (
        jnp.arange(outer_size, dtype=jnp.int32)[:, None]
        * jnp.arange(inner_size, dtype=jnp.int32)[None, :]
        % (outer_size * inner_size)
    )
    angles = product.astype(jnp.float32) * (direction * 2.0 * math.pi / (outer_size * inner_size))
    return (jnp.cos(angles), jnp.sin(angles))


def rotate(values, cosine, sine_part):
    return jnp.stack(
        [values[0] * cosine - values[1] * sine_part, values[0] * sine_part + values[1] * cosine]
    )


def spectral_core(values, phases):
    outer_size = values.shape[-2]
    inner_size = values.shape[-1]
    values = jnp.einsum("pqkn,q...nm->p...km", dft_table(outer_size, -1), values, precision=HIGHEST)
    cos_part, sin_part = twiddle(outer_size, inner_size, -1)
    values = rotate(values, cos_part, sin_part)
    values = jnp.einsum("pqjm,q...km->p...kj", dft_table(inner_size, -1), values, precision=HIGHEST)
    phase_grid = phases.reshape(inner_size, outer_size).T
    values = rotate(values, jnp.cos(phase_grid), jnp.sin(phase_grid))
    values = jnp.einsum("pqmj,q...kj->p...km", dft_table(inner_size, 1), values, precision=HIGHEST)
    cos_part, sin_part = twiddle(outer_size, inner_size, 1)
    return rotate(values, cos_part, sin_part)


def azimuth_compress(values, phases):
    length = values.shape[-1]
    inner_size = 128
    outer_size = length // inner_size
    spectrum = spectral_core(values.reshape(values.shape[:-1] + (outer_size, inner_size)), phases)
    result = (
        jnp.einsum("pqnk,q...km->p...nm", dft_table(outer_size, 1), spectrum, precision=HIGHEST)
        / length
    )
    return result.reshape(values.shape)


def range_compress(values, phases, row_count):
    length = values.shape[-1]
    inner_size = 128
    outer_size = length // inner_size
    spectrum = spectral_core(values.reshape(values.shape[:-1] + (outer_size, inner_size)), phases)
    inverse_rows = dft_table(outer_size, 1)
    result = jnp.einsum("pqnk,qdlkm->pdnml", inverse_rows, spectrum, precision=HIGHEST) / length
    return result.reshape(2, values.shape[1], row_count * inner_size, values.shape[2])


def running_window(values):
    width = 2 * WIN_HALF + 1
    count = values.shape[-1]
    level = jnp.pad(values, ((0, 0), (0, 0), (WIN_HALF, WIN_HALF)))
    total = jnp.zeros_like(values)
    offset = 0
    span = 1
    while span <= width:
        if width & span:
            total = total + level[..., offset : offset + count]
            offset = offset + span
        level = level[..., :-span] + level[..., span:]
        span = span * 2
    return total


def link_block(real_ext, imag_ext, valid_mask):
    date_count = real_ext.shape[0]
    pair_list = [
        (former, latter) for former in range(date_count) for latter in range(former + 1, date_count)
    ]
    terms = [
        real_ext[former] * real_ext[former] + imag_ext[former] * imag_ext[former]
        for former in range(date_count)
    ]
    for former, latter in pair_list:
        terms.append(real_ext[former] * real_ext[latter] + imag_ext[former] * imag_ext[latter])
        terms.append(imag_ext[former] * real_ext[latter] - real_ext[former] * imag_ext[latter])
    stacked = jnp.stack(terms)
    across = stacked[:, :-2] + stacked[:, 1:-1] + stacked[:, 2:]
    window = running_window(across)
    window = window / (3 * (2 * WIN_HALF + 1))
    powers = window[:date_count] + 1e-06
    coherence = {}
    for number, pair in enumerate(pair_list):
        factor = lax.rsqrt(powers[pair[0]] * powers[pair[1]])
        coherence[pair] = (
            window[date_count + 2 * number] * factor,
            window[date_count + 2 * number + 1] * factor,
        )
    vector_real = [jnp.ones_like(powers[0]) for former in range(date_count)]
    vector_imag = [jnp.zeros_like(powers[0]) for former in range(date_count)]
    for iteration in range(POWER_ITERS):
        new_real = []
        new_imag = []
        for target in range(date_count):
            acc_real = vector_real[target]
            acc_imag = vector_imag[target]
            for source in range(date_count):
                if source != target:
                    if target < source:
                        part_real, part_imag = coherence[target, source]
                    else:
                        part_real, part_imag = coherence[source, target]
                        part_imag = -part_imag
                    acc_real = (
                        acc_real + part_real * vector_real[source] - part_imag * vector_imag[source]
                    )
                    acc_imag = (
                        acc_imag + part_real * vector_imag[source] + part_imag * vector_real[source]
                    )
            new_real.append(acc_real)
            new_imag.append(acc_imag)
        mean_square = (
            sum(
                (
                    new_real[target] * new_real[target] + new_imag[target] * new_imag[target]
                    for target in range(date_count)
                )
            )
            / date_count
        )
        factor = lax.rsqrt(jnp.maximum(mean_square, 1.0))
        vector_real = [entry * factor for entry in new_real]
        vector_imag = [entry * factor for entry in new_imag]
    magnitude = sum(
        (
            jnp.sqrt(
                coherence[pair][0] * coherence[pair][0] + coherence[pair][1] * coherence[pair][1]
            )
            for pair in pair_list
        )
    ) / len(pair_list)
    quality = valid_mask[:, None] * (0.05 + magnitude)
    vector = jnp.stack([jnp.stack(vector_real), jnp.stack(vector_imag)])
    return (vector, quality)


def shards(raw_echoes, range_phase, azimuth_phase, calibration):
    groups = lax.axis_size("date")
    group_dates = raw_echoes.shape[1]
    local_lines = raw_echoes.shape[2]
    length = raw_echoes.shape[3]
    outer_size = length // 128
    ranged = range_compress(raw_echoes.astype(jnp.float32), range_phase, outer_size)
    ranged = ranged.reshape(2, group_dates, groups, length // groups, local_lines)
    turned = one_exchange(ranged, ("date", "strip"), ("date", "strip"), (2, 3), (1, 4))
    focused = azimuth_compress(turned, azimuth_phase)
    all_dates = group_dates * groups
    column_count = calibration.shape[1]
    line_count = focused.shape[-1]
    image = focused.reshape(2, all_dates, column_count, line_count) * calibration[None, :, :, None]
    halo = 1 + SMOOTH_PASSES
    extended = extended_2(image, ((("date", "strip"), 2),), halo)
    total_columns = column_count * lax.axis_size("date") * lax.axis_size("strip")
    first = lax.axis_index(("date", "strip")) * column_count - SMOOTH_PASSES
    columns = first + jnp.arange(column_count + 2 * SMOOTH_PASSES, dtype=jnp.int32)
    valid_mask = ((columns >= 0) & (columns < total_columns)).astype(jnp.float32)
    vector, quality = link_and_smooth(extended, valid_mask)
    return (vector, quality)


def solution(mesh):
    in_specs = (P(None, "date", "strip", None), P(), P(), P(None, ("date", "strip")))
    out_specs = (P(None, None, ("date", "strip"), None), P(("date", "strip"), None))
    return jax.shard_map(shards, mesh=mesh, in_specs=in_specs, out_specs=out_specs, check_vma=False)
```

profile of v0, /device:TPU:31, one launch (start us, length us, event | category | flops | bytes accessed | tf_op | source)
XLA Modules:
  0.0 172.9 jit_solution(4960622761196616460)
XLA Ops:
  0.8 0.3 multiply_sine_fusion.1
  1.1 0.3 fusion.37
  1.3 0.3 multiply_sine_fusion
  1.6 0.3 fusion.38
  2.0 0.1 fusion.56
  2.1 1.1 copy.92
  3.2 0.7 fusion.67
  3.9 0.1 cos.132
  4.1 0.1 sin.156
  4.2 0.6 convolution_bitcast_fusion
  4.9 0.1 multiply_subtract_fusion.5
  5.0 1.0 convolution_bitcast_fusion.7
  6.1 0.1 multiply_subtract_fusion.4
  6.2 1.0 convolution_bitcast_fusion.6
  7.3 0.1 multiply_subtract_fusion.3
  7.4 1.0 fusion.3
  8.4 0.5 reshape_reshape_reshape.3
  9.0 0.8 copy.52
  9.8 1.0 copy.53
  10.8 1.8 %copy.54 = f32[256,2,2,1,4,64]{5,4,3,2,1,0:T(4,128)S(1)} copy(f32[256,2,2,1,4,64]{0,3,5,4,2,1:T(1,128)S(1)} %bitcast.181) | data formatting | bytes 2097152 | tf_op jit(solution)/shard_map/reshape | solution.py:183
  12.7 2.9 %reshape.592 = f32[256,1,1024]{2,1,0:T(1,128)} reshape(f32[256,2,2,1,4,64]{5,4,3,2,1,0:T(4,128)S(1)} %copy.54) | data formatting | bytes 2097152
  15.6 14.7 %all-to-all-start = ((f32[256,1,1024]{2,1,0:T(1,128)}), f32[256,1,1024]{2,1,0:T(1,128)S(1)}, u32[]{:S(2)}, u32[]{:S(2)}) async-start(f32[256,1,1024]{2,1,0:T(1,128)} %reshape.592), calls=%async_computation | async-start | bytes 2097152 | tf_op jit(solution)/shard_map/all_to_all | solution.py:184
  30.3 0.1 fusion.66
  30.4 0.1 cos.140
  30.5 0.7 copy.59
  31.2 0.1 sin.164
  31.2 0.7 copy.60
  31.9 0.1 fusion.43
  32.1 0.1 fusion.44
  32.2 0.1 multiply_sine_fusion.5
  32.4 0.8 multiply_sine_fusion.4
  33.2 0.8 multiply_sine_fusion.3
  33.9 0.1 multiply_sine_fusion.2
  34.1 0.7 maximum_bitcast_fusion.25
  34.8 0.7 maximum_bitcast_fusion.27
  35.4 22.3 %all-to-all-done = f32[256,1,1024]{2,1,0:T(1,128)S(1)} async-done(((f32[256,1,1024]{2,1,0:T(1,128)}), f32[256,1,1024]{2,1,0:T(1,128)S(1)}, u32[]{:S(2)}, u32[]{:S(2)}) %all-to-all-start) | async-done | bytes 1048608 | tf_op jit(solution)/shard_map/all_to_all | solution.py:184
  57.7 0.5 broadcast.961
  58.2 3.1 %reduce = f32[256,1024]{1,0:T(8,128)S(1)} reduce(f32[256,1,1024]{2,1,0:T(1,128)S(1)} %all-to-all-done, f32[]{:T(128)} %broadcast.961), dimensions={1}, to_apply=%all_to_all.3.reduce_sub_computation | reduce | bytes 2097156 | tf_op jit(solution)/shard_map/all_to_all | solution.py:184
  61.3 1.4 reshape.593
  62.7 1.2 copy.55
  64.0 1.1 copy.56
  65.1 1.8 %copy.89 = f32[2,4,1,4,128,64]{5,4,0,3,1,2:T(8,128)S(1)} copy(f32[2,4,1,4,128,64]{4,5,3,2,1,0:T(8,128)} %bitcast.183) | data formatting | bytes 2097152 | tf_op jit(solution)/shard_map/reshape
  66.9 0.3 reshape.579
  67.3 2.0 %convolution_bitcast_fusion.4 = f32[2,4,1,4,64,128]{5,4,0,3,1,2:T(8,128)S(1)} fusion(f32[2,4,4,64,128,1]{4,3,0,2,1,5:T(8,128)S(1)} %reshape.579, f32[1,2,64,64]{3,2,1,0:T(8,128)} %get-tuple-element.25, f32[1,2,64,64]{3,2,1,0:T(8,128)} %get-tuple-element.24), kind=kOutput, calls=%fused_computation.7 | convolution fusion | flops 402669568 | bytes 2162688 | tf_op jit(solution)/shard_map/pqkn,q...nm->p...km/dot_general | solution.py:237
  69.3 0.9 multiply_subtract_fusion.2
  70.3 1.0 convolution_bitcast_fusion.3
  71.4 0.2 multiply_subtract_fusion.1
  71.6 1.0 convolution_bitcast_fusion.2
  72.6 0.2 multiply_subtract_fusion
  72.8 1.1 fusion.1
  73.9 0.6 reshape.591
  74.5 0.7 copy_multiply_fusion
  75.2 0.5 fusion.65
  75.7 0.5 copy.62
  76.2 6.9 %collective-permute-start = (f32[2,4,3,8192]{3,1,2,0:T(4,128)S(1)}, f32[2,4,3,8192]{3,1,2,0:T(4,128)S(1)}, u32[]{:S(2)}, u32[]{:S(2)}) collective-permute-start(f32[2,4,3,8192]{3,1,2,0:T(4,128)S(1)} %copy.62), channel_id=1, source_target_pairs={{0,1},{1,2},{2,3},{3,4},{4,5},{5,6},{6,7},{7,8},{8,9},{9,10},{10,1... | collective-permute-start | bytes 2359304 | tf_op jit(solution)/shard_map/ppermute | solution.py:197
  83.1 0.5 copy.63
  83.7 1.9 %collective-permute-start.1 = (f32[2,4,3,8192]{3,1,2,0:T(4,128)S(1)}, f32[2,4,3,8192]{3,1,2,0:T(4,128)}, u32[]{:S(2)}, u32[]{:S(2)}) collective-permute-start(f32[2,4,3,8192]{3,1,2,0:T(4,128)S(1)} %copy.63), channel_id=1, source_target_pairs={{1,0},{2,1},{3,2},{4,3},{5,4},{6,5},{7,6},{8,7},{9,8},{10,9},{11,1... | collective-permute-start | bytes 2359304 | tf_op jit(solution)/shard_map/ppermute | solution.py:198
  85.6 6.4 %collective-permute-done = f32[2,4,3,8192]{3,1,2,0:T(4,128)S(1)} collective-permute-done((f32[2,4,3,8192]{3,1,2,0:T(4,128)S(1)}, f32[2,4,3,8192]{3,1,2,0:T(4,128)S(1)}, u32[]{:S(2)}, u32[]{:S(2)}) %collective-permute-start) | collective-permute-done | bytes 786464 | tf_op jit(solution)/shard_map/ppermute | solution.py:197
  92.1 0.5 copy.64
  92.6 8.7 %collective-permute-done.1 = f32[2,4,3,8192]{3,1,2,0:T(4,128)} collective-permute-done((f32[2,4,3,8192]{3,1,2,0:T(4,128)S(1)}, f32[2,4,3,8192]{3,1,2,0:T(4,128)}, u32[]{:S(2)}, u32[]{:S(2)}) %collective-permute-start.1) | collective-permute-done | bytes 786464 | tf_op jit(solution)/shard_map/ppermute | solution.py:198
  101.3 1.7 copy.65
  103.0 2.9 %pad_maximum_fusion.prev_ref.cur_ref.next_ref = f32[2,4,10,8192]{3,2,1,0:T(8,128)} fusion(f32[2,4,3,8192]{3,2,1,0:T(4,128)S(1)} %copy.65, f32[2,4,4,8192]{3,2,1,0:T(4,128)S(1)} %copy_multiply_fusion, f32[2,4,3,8192]{3,2,1,0:T(4,128)S(1)} %copy.64), kind=kLoop, calls=%fused_computation | loop fusion | flops 1310720 | bytes 5242880 | tf_op jit(solution)/shard_map/concatenate | solution.py:204
  105.9 0.7 broadcast_in_dim.2.mask_ref
  106.5 66.3 %shard_map.59 = (f32[2,4,4,8192]{3,2,1,0:T(4,128)}, f32[4,8192]{1,0:T(4,128)}) custom-call(f32[8,128]{1,0:T(8,128)} %broadcast_in_dim.2.mask_ref, f32[2,4,10,8192]{3,2,1,0:T(8,128)} %pad_maximum_fusion.prev_ref.cur_ref.next_ref, f32[2,4,10,8192]{3,2,1,0:T(8,128)} %pad_maximum_fusion.prev_ref.cur_ref.next_ref, ...), custom_call_target="tpu_custom_call" | custom-call | tf_op jit(solution)/shard_map/pallas_call | solution.py:142
  (32 shorter events, 0.5 us)
Async XLA Ops:
  6.2 1.2 copy-start
  12.7 17.6 %copy-start.8 = (f32[8192]{0:T(1024)S(1)}, f32[8192]{0:T(1024)}, u32[]{:S(2)}) copy-start(f32[8192]{0:T(1024)} %param.6) | copy-start | bytes 98308
  15.6 42.1 %all-to-all-start = ((f32[256,1,1024]{2,1,0:T(1,128)}), f32[256,1,1024]{2,1,0:T(1,128)S(1)}, u32[]{:S(2)}, u32[]{:S(2)}) async-start(f32[256,1,1024]{2,1,0:T(1,128)} %reshape.592), calls=%async_computation | async-start | bytes 2097152 | tf_op jit(solution)/shard_map/all_to_all | solution.py:184
  67.3 4.1 %copy-start.4 = (f32[64,128]{1,0:T(8,128)S(1)}, f32[64,128]{1,0:T(8,128)}, u32[]{:S(2)}) copy-start(f32[64,128]{1,0:T(8,128)} %copy.59) | copy-start | bytes 98308
  67.3 4.1 %copy-start.5 = (f32[64,128]{1,0:T(8,128)S(1)}, f32[64,128]{1,0:T(8,128)}, u32[]{:S(2)}) copy-start(f32[64,128]{1,0:T(8,128)} %copy.60) | copy-start | bytes 98308
  67.3 4.2 %copy-start.1 = (f32[1,2,128,128]{3,2,1,0:T(8,128)S(1)}, f32[1,2,128,128]{3,2,1,0:T(8,128)}, u32[]{:S(2)}) copy-start(f32[1,2,128,128]{3,2,1,0:T(8,128)} %copy-done) | copy-start | bytes 393220
  69.3 3.3 %copy-start.6 = (f32[64,128]{1,0:T(8,128)S(1)}, f32[64,128]{1,0:T(8,128)}, u32[]{:S(2)}) copy-start(f32[64,128]{1,0:T(8,128)} %get-tuple-element.48) | copy-start | bytes 98308
  69.3 3.3 %copy-start.7 = (f32[64,128]{1,0:T(8,128)S(1)}, f32[64,128]{1,0:T(8,128)}, u32[]{:S(2)}) copy-start(f32[64,128]{1,0:T(8,128)} %get-tuple-element.49) | copy-start | bytes 98308
  70.3 2.5 %copy-start.2 = (f32[1,2,64,64]{3,2,1,0:T(8,128)S(1)}, f32[1,2,64,64]{3,2,1,0:T(8,128)}, u32[]{:S(2)}) copy-start(f32[1,2,64,64]{3,2,1,0:T(8,128)} %get-tuple-element.20) | copy-start | bytes 98308
  70.3 2.5 %copy-start.3 = (f32[1,2,64,64]{3,2,1,0:T(8,128)S(1)}, f32[1,2,64,64]{3,2,1,0:T(8,128)}, u32[]{:S(2)}) copy-start(f32[1,2,64,64]{3,2,1,0:T(8,128)} %get-tuple-element.21) | copy-start | bytes 98308
  71.5 3.0 %copy-start.9 = (f32[4,4]{1,0:T(4,128)S(1)}, f32[4,4]{1,0:T(4,128)}, u32[]{:S(2)}) copy-start(f32[4,4]{1,0:T(4,128)} %param.7) | copy-start | bytes 196
  76.2 15.8 %collective-permute-start = (f32[2,4,3,8192]{3,1,2,0:T(4,128)S(1)}, f32[2,4,3,8192]{3,1,2,0:T(4,128)S(1)}, u32[]{:S(2)}, u32[]{:S(2)}) collective-permute-start(f32[2,4,3,8192]{3,1,2,0:T(4,128)S(1)} %copy.62), channel_id=1, source_target_pairs={{0,1},{1,2},{2,3},{3,4},{4,5},{5,6},{6,7},{7,8},{8,9},{9,10},{10,1... | collective-permute-start | bytes 2359304 | tf_op jit(solution)/shard_map/ppermute | solution.py:197
  83.7 17.6 %collective-permute-start.1 = (f32[2,4,3,8192]{3,1,2,0:T(4,128)S(1)}, f32[2,4,3,8192]{3,1,2,0:T(4,128)}, u32[]{:S(2)}, u32[]{:S(2)}) collective-permute-start(f32[2,4,3,8192]{3,1,2,0:T(4,128)S(1)} %copy.63), channel_id=1, source_target_pairs={{1,0},{2,1},{3,2},{4,3},{5,4},{6,5},{7,6},{8,7},{9,8},{10,9},{11,1... | collective-permute-start | bytes 2359304 | tf_op jit(solution)/shard_map/ppermute | solution.py:198
where the time goes:
time: 173 us
  Pallas kernels  66.3 us (38%)
  waiting for transfers between devices  37.4 us (22%)
  starting transfers between devices  23.5 us (14%)
  local copies, waits for them, and re-layouts  22.4 us (13%)
  other arithmetic  13.3 us (8%)
  matrix products  8.85 us (5%)
    pallas_call x1, Pallas kernels, link_and_smooth(): pl.pallas_call(link_kernel, grid=(steps,), in_specs=[pl.BlockSpec((rows,...  66.3 us
    all_to_all x1, waiting for transfers between devices, one_exchange(): tiles = lax.all_to_all(tiles, axis, split_axis=0, concat_axis=0, tiled=True)  22.3 us
    all_to_all x1, starting transfers between devices, one_exchange(): tiles = lax.all_to_all(tiles, axis, split_axis=0, concat_axis=0, tiled=True)  14.7 us
    ppermute x1, waiting for transfers between devices, extended_2(): lax.ppermute(first, axis, [(b, a) for a, b in up])  8.69 us
    ppermute x1, starting transfers between devices, extended_2(): lax.ppermute(last, axis, up)  6.9 us
    ppermute x1, waiting for transfers between devices, extended_2(): lax.ppermute(last, axis, up)  6.45 us
    unnamed x23, local copies, waits for them, and re-layouts  5.47 us
  transfers between devices with their start and end apart: 3, of which 3 were waited for; matrix products, arithmetic and copies ran while one was open for 4% of the time, Pallas kernels for 0%

commit v1 on v0

--- a/solution.py
+++ b/solution.py
@@ -13,63 +13,59 @@
 
 
 HIGHEST = lax.Precision.HIGHEST
-BLOCK = 512
+BLOCK = 1024
 EDGE = 128
 CHUNK = 128
-
-
-def window_lines(values):
-    ones = values + pltpu.roll(values, 1, 1)
-    twos = ones + pltpu.roll(ones, 2, 1)
-    fours = twos + pltpu.roll(twos, 4, 1)
-    eights = fours + pltpu.roll(fours, 8, 1)
-    width = values.shape[1]
-    return (
-        pltpu.roll(eights, width - WIN_HALF, 1)
-        + pltpu.roll(twos, 5, 1)
-        + pltpu.roll(ones, 9, 1)
-        + pltpu.roll(values, WIN_HALF, 1)
-    )
-
-
-def link_kernel(mask_ref, prev_ref, cur_ref, next_ref, vec_ref, qual_ref, image, sums):
+ROWS = 8
+
+
+def link_kernel(mask_ref, band_ref, prev_ref, cur_ref, next_ref, vec_ref, qual_ref, image, terms, high, low, sums):
     step = pl.program_id(0)
     last = pl.num_programs(0) - 1
     dates = cur_ref.shape[1]
     block = cur_ref.shape[3]
+    padded = cur_ref.shape[2]
     image[:, :, :, EDGE : EDGE + block] = cur_ref[...]
     image[:, :, :, :EDGE] = jnp.where(step > 0, prev_ref[...], 0.0)
     image[:, :, :, EDGE + block :] = jnp.where(step < last, next_ref[...], 0.0)
-    rows = sums.shape[1]
     pairs = [(a, b) for a in range(dates) for b in range(a + 1, dates)]
-
-    def part(p, d, shift):
-        return image[p, d, pl.ds(shift, rows), :]
-
-    def term(kind, a, b, shift):
-        ra, ia = part(0, a, shift), part(1, a, shift)
-        if kind == 0:
-            return ra * ra + ia * ia
-        rb, ib = part(0, b, shift), part(1, b, shift)
-        if kind == 1:
-            return ra * rb + ia * ib
-        return ia * rb - ra * ib
-
     specs = [(0, a, a) for a in range(dates)]
     for a, b in pairs:
         specs.append((1, a, b))
         specs.append((2, a, b))
+
     for number, (kind, a, b) in enumerate(specs):
-        across = term(kind, a, b, 0) + term(kind, a, b, 1) + term(kind, a, b, 2)
-        total = window_lines(across)
-        sums[number] = total[:, EDGE : EDGE + block]
+        ra, ia = image[0, a], image[1, a]
+        if kind == 0:
+            value = ra * ra + ia * ia
+        else:
+            rb, ib = image[0, b], image[1, b]
+            if kind == 1:
+                value = ra * rb + ia * ib
+            else:
+                value = ia * rb - ra * ib
+        across = value + pltpu.roll(value, padded - 1, 0) + pltpu.roll(value, padded - 2, 0)
+        terms[number * ROWS : (number + 1) * ROWS, :] = across[:ROWS]
+    full = terms[...]
+    top = full.astype(jnp.bfloat16)
+    high[...] = top
+    low[...] = (full - top.astype(jnp.float32)).astype(jnp.bfloat16)
+    band = band_ref[...]
+    for index in range(block // CHUNK):
+        left = index * CHUNK
+        window = jnp.dot(high[:, left : left + CHUNK + 2 * EDGE], band, preferred_element_type=jnp.float32)
+        window = window + jnp.dot(low[:, left : left + CHUNK + 2 * EDGE], band, preferred_element_type=jnp.float32)
+        sums[:, left : left + CHUNK] = window
 
     mask = mask_ref[...]
-    scale = 3 * (2 * WIN_HALF + 1)
+    inverse_scale = 1.0 / (3 * (2 * WIN_HALF + 1))
 
     def chunk_body(index, carry):
         start = pl.multiple_of(index * CHUNK, CHUNK)
-        window = [sums[number, :, pl.ds(start, CHUNK)] / scale for number in range(len(specs))]
+        window = [
+            sums[number * ROWS : (number + 1) * ROWS, pl.ds(start, CHUNK)] * inverse_scale
+            for number in range(len(specs))
+        ]
         powers = [window[a] + 1e-06 for a in range(dates)]
         coherence = {}
         for number, (a, b) in enumerate(pairs):
@@ -78,35 +74,43 @@
                 window[dates + 2 * number] * factor,
                 window[dates + 2 * number + 1] * factor,
             )
-        vector_real = [jnp.ones_like(powers[0]) for _ in range(dates)]
-        vector_imag = [jnp.zeros_like(powers[0]) for _ in range(dates)]
+
+        def entry(target, source):
+            if target < source:
+                return coherence[target, source]
+            part_real, part_imag = coherence[source, target]
+            return part_real, -part_imag
+
+        new_real = []
+        new_imag = []
+        for target in range(dates):
+            sources = [entry(target, source) for source in range(dates) if source != target]
+            new_real.append(1.0 + sum(part[0] for part in sources))
+            new_imag.append(sum(part[1] for part in sources))
         for iteration in range(POWER_ITERS):
-            new_real = []
-            new_imag = []
-            for target in range(dates):
-                acc_real = vector_real[target]
-                acc_imag = vector_imag[target]
-                for source in range(dates):
-                    if source != target:
-                        if target < source:
-                            part_real, part_imag = coherence[target, source]
-                        else:
-                            part_real, part_imag = coherence[source, target]
-                            part_imag = -part_imag
-                        acc_real = (
-                            acc_real + part_real * vector_real[source] - part_imag * vector_imag[source]
-                        )
-                        acc_imag = (
-                            acc_imag + part_real * vector_imag[source] + part_imag * vector_real[source]
-                        )
-                new_real.append(acc_real)
-                new_imag.append(acc_imag)
+            if iteration > 0:
+                new_real = []
+                new_imag = []
+                for target in range(dates):
+                    acc_real = vector_real[target]
+                    acc_imag = vector_imag[target]
+                    for source in range(dates):
+                        if source != target:
+                            part_real, part_imag = entry(target, source)
+                            acc_real = (
+                                acc_real + part_real * vector_real[source] - part_imag * vector_imag[source]
+                            )
+                            acc_imag = (
+                                acc_imag + part_real * vector_imag[source] + part_imag * vector_real[source]
+                            )
+                    new_real.append(acc_real)
+                    new_imag.append(acc_imag)
             mean_square = (
                 sum(new_real[t] * new_real[t] + new_imag[t] * new_imag[t] for t in range(dates)) / dates
             )
             factor = lax.rsqrt(jnp.maximum(mean_square, 1.0))
-            vector_real = [entry * factor for entry in new_real]
-            vector_imag = [entry * factor for entry in new_imag]
+            vector_real = [value * factor for value in new_real]
+            vector_imag = [value * factor for value in new_imag]
         magnitude = sum(
             jnp.sqrt(coherence[pair][0] * coherence[pair][0] + coherence[pair][1] * coherence[pair][1])
             for pair in pairs
@@ -114,17 +118,17 @@
         quality = mask * (0.05 + magnitude)
         vectors = vector_real + vector_imag
         for passes in range(SMOOTH_PASSES):
-            denominator = quality + pltpu.roll(quality, 1, 0) + pltpu.roll(quality, rows - 1, 0)
-            denominator = jnp.where(denominator > 0, denominator, 1.0)
+            denominator = quality + pltpu.roll(quality, 1, 0) + pltpu.roll(quality, ROWS - 1, 0)
+            inverse = 1.0 / jnp.where(denominator > 0, denominator, 1.0)
             smoothed = []
-            for entry in vectors:
-                weighted = entry * quality
-                numerator = weighted + pltpu.roll(weighted, 1, 0) + pltpu.roll(weighted, rows - 1, 0)
-                smoothed.append(numerator / denominator)
+            for value in vectors:
+                weighted = value * quality
+                numerator = weighted + pltpu.roll(weighted, 1, 0) + pltpu.roll(weighted, ROWS - 1, 0)
+                smoothed.append(numerator * inverse)
             vectors = smoothed
-        keep = slice(SMOOTH_PASSES, rows - SMOOTH_PASSES)
-        for number, entry in enumerate(vectors):
-            vec_ref[number // dates, number % dates, :, pl.ds(start, CHUNK)] = entry[keep]
+        keep = slice(SMOOTH_PASSES, ROWS - SMOOTH_PASSES)
+        for number, value in enumerate(vectors):
+            vec_ref[number // dates, number % dates, :, pl.ds(start, CHUNK)] = value[keep]
         qual_ref[:, pl.ds(start, CHUNK)] = quality[keep]
         return carry
 
@@ -133,20 +137,28 @@
 
 def link_and_smooth(extended, valid_mask):
     parts, dates, columns, lines = extended.shape
-    rows = columns - 2
-    kept = rows - 2 * SMOOTH_PASSES
+    padded = 16
+    extended = jnp.concatenate(
+        [extended, jnp.zeros((parts, dates, padded - columns, lines), extended.dtype)], axis=2
+    )
+    kept = ROWS - 2 * SMOOTH_PASSES
     steps = lines // BLOCK
     per_block = BLOCK // EDGE
     edges = lines // EDGE
-    mask = jnp.broadcast_to(valid_mask[:, None], (rows, CHUNK))
+    term_count = dates + dates * (dates - 1)
+    mask = jnp.broadcast_to(valid_mask[:, None], (ROWS, CHUNK))
+    offset = jnp.arange(CHUNK + 2 * EDGE, dtype=jnp.int32)[:, None] - EDGE - jnp.arange(CHUNK, dtype=jnp.int32)[None, :]
+    band = (jnp.abs(offset) <= WIN_HALF).astype(jnp.bfloat16)
+    width = BLOCK + 2 * EDGE
     return pl.pallas_call(
         link_kernel,
         grid=(steps,),
         in_specs=[
-            pl.BlockSpec((rows, CHUNK), lambda i: (0, 0)),
-            pl.BlockSpec((parts, dates, columns, EDGE), lambda i: (0, 0, 0, jnp.maximum(i * per_block - 1, 0))),
-            pl.BlockSpec((parts, dates, columns, BLOCK), lambda i: (0, 0, 0, i)),
-            pl.BlockSpec((parts, dates, columns, EDGE), lambda i: (0, 0, 0, jnp.minimum((i + 1) * per_block, edges - 1))),
+            pl.BlockSpec((ROWS, CHUNK), lambda i: (0, 0)),
+            pl.BlockSpec((CHUNK + 2 * EDGE, CHUNK), lambda i: (0, 0)),
+            pl.BlockSpec((parts, dates, padded, EDGE), lambda i: (0, 0, 0, jnp.maximum(i * per_block - 1, 0))),
+            pl.BlockSpec((parts, dates, padded, BLOCK), lambda i: (0, 0, 0, i)),
+            pl.BlockSpec((parts, dates, padded, EDGE), lambda i: (0, 0, 0, jnp.minimum((i + 1) * per_block, edges - 1))),
         ],
         out_specs=[
             pl.BlockSpec((parts, dates, kept, BLOCK), lambda i: (0, 0, 0, i)),
@@ -157,10 +169,13 @@
             jax.ShapeDtypeStruct((kept, lines), jnp.float32),
         ],
         scratch_shapes=[
-            pltpu.VMEM((parts, dates, columns, BLOCK + 2 * EDGE), jnp.float32),
-            pltpu.VMEM((dates + dates * (dates - 1), rows, BLOCK), jnp.float32),
+            pltpu.VMEM((parts, dates, padded, width), jnp.float32),
+            pltpu.VMEM((term_count * ROWS, width), jnp.float32),
+            pltpu.VMEM((term_count * ROWS, width), jnp.bfloat16),
+            pltpu.VMEM((term_count * ROWS, width), jnp.bfloat16),
+            pltpu.VMEM((term_count * ROWS, BLOCK), jnp.float32),
         ],
-    )(mask, extended, extended, extended)
+    )(mask, band, extended, extended, extended)
 
 
 def split_up(x, dim, count):

time: 173 us -> 128 us (0.74)
  Pallas kernels: 66.3 us -> 20.5 us
    pallas_call x1, Pallas kernels: 66.3 us -> 20.5 us  [link_and_smooth(): pl.pallas_call(link_kernel, grid=(steps,), in_specs=[pl.BlockSpec((ROWS,...]
  transfers between devices with their start and end apart: 3 -> 3, of which waited for: 3 -> 3; matrix products, arithmetic and copies ran while one was open for 4% -> 6% of each run, Pallas kernels for 0% -> 0%
where the time goes in v1:
time: 128 us; the launch traced here: 127 us
  waiting for transfers between devices  36.6 us (29%)
  starting transfers between devices  23.5 us (18%)
  local copies, waits for them, and re-layouts  22.4 us (18%)
  Pallas kernels  20.5 us (16%)
  other arithmetic  14.2 us (11%)
  matrix products  8.85 us (7%)
    all_to_all x1, waiting for transfers between devices, one_exchange(): tiles = lax.all_to_all(tiles, axis, split_axis=0, concat_axis=0, tiled=True)  22.3 us
    pallas_call x1, Pallas kernels, link_and_smooth(): pl.pallas_call(link_kernel, grid=(steps,), in_specs=[pl.BlockSpec((ROWS,...  20.5 us
    all_to_all x1, starting transfers between devices, one_exchange(): tiles = lax.all_to_all(tiles, axis, split_axis=0, concat_axis=0, tiled=True)  14.7 us
    ppermute x1, waiting for transfers between devices, extended_2(): lax.ppermute(first, axis, [(b, a) for a, b in up])  8.69 us
    ppermute x1, starting transfers between devices, extended_2(): lax.ppermute(last, axis, up)  6.9 us
    ppermute x1, waiting for transfers between devices, extended_2(): lax.ppermute(last, axis, up)  5.61 us
    unnamed x23, local copies, waits for them, and re-layouts  5.47 us
    all_to_all x1, other arithmetic, one_exchange(): tiles = lax.all_to_all(tiles, axis, split_axis=0, concat_axis=0, tiled=True)  3.13 us
  transfers between devices with their start and end apart: 3, of which 3 were waited for; matrix products, arithmetic and copies ran while one was open for 6% of the time, Pallas kernels for 0%

profile of v1, /device:TPU:31, one launch (start us, length us, event | category | flops | bytes accessed | tf_op | source)
XLA Modules:
  0.0 127.1 jit_solution(1313488662815672955)
XLA Ops:
  0.8 0.3 multiply_sine_fusion.1
  1.1 0.3 fusion.38
  1.3 0.3 multiply_sine_fusion
  1.6 0.3 fusion.39
  2.1 1.1 copy.92
  3.2 0.7 fusion.68
  3.9 0.1 cos.132
  4.1 0.1 sin.156
  4.2 0.6 convolution_bitcast_fusion
  4.9 0.1 multiply_subtract_fusion.5
  5.0 1.0 convolution_bitcast_fusion.7
  6.1 0.1 multiply_subtract_fusion.4
  6.2 1.0 convolution_bitcast_fusion.6
  7.3 0.1 multiply_subtract_fusion.3
  7.4 1.0 fusion.3
  8.4 0.5 reshape_reshape_reshape.3
  9.0 0.8 copy.52
  9.8 1.0 copy.53
  10.8 1.8 %copy.54 = f32[256,2,2,1,4,64]{5,4,3,2,1,0:T(4,128)S(1)} copy(f32[256,2,2,1,4,64]{0,3,5,4,2,1:T(1,128)S(1)} %bitcast.181) | data formatting | bytes 2097152 | tf_op jit(solution)/shard_map/reshape | solution.py:198
  12.7 2.9 %reshape.597 = f32[256,1,1024]{2,1,0:T(1,128)} reshape(f32[256,2,2,1,4,64]{5,4,3,2,1,0:T(4,128)S(1)} %copy.54) | data formatting | bytes 2097152
  15.6 14.7 %all-to-all-start = ((f32[256,1,1024]{2,1,0:T(1,128)}), f32[256,1,1024]{2,1,0:T(1,128)S(1)}, u32[]{:S(2)}, u32[]{:S(2)}) async-start(f32[256,1,1024]{2,1,0:T(1,128)} %reshape.597), calls=%async_computation | async-start | bytes 2097152 | tf_op jit(solution)/shard_map/all_to_all | solution.py:199
  30.3 0.1 fusion.67
  30.4 0.1 cos.140
  30.5 0.7 copy.59
  31.2 0.7 copy.60
  31.9 0.1 fusion.44
  32.1 0.1 fusion.45
  32.2 0.1 multiply_sine_fusion.5
  32.4 0.8 multiply_sine_fusion.4
  33.2 0.8 multiply_sine_fusion.3
  33.9 0.1 multiply_sine_fusion.2
  34.1 0.7 maximum_bitcast_fusion.25
  34.8 0.7 maximum_bitcast_fusion.27
  35.4 22.3 %all-to-all-done = f32[256,1,1024]{2,1,0:T(1,128)S(1)} async-done(((f32[256,1,1024]{2,1,0:T(1,128)}), f32[256,1,1024]{2,1,0:T(1,128)S(1)}, u32[]{:S(2)}, u32[]{:S(2)}) %all-to-all-start) | async-done | bytes 1048608 | tf_op jit(solution)/shard_map/all_to_all | solution.py:199
  57.7 0.5 broadcast.973
  58.2 3.1 %reduce = f32[256,1024]{1,0:T(8,128)S(1)} reduce(f32[256,1,1024]{2,1,0:T(1,128)S(1)} %all-to-all-done, f32[]{:T(128)} %broadcast.973), dimensions={1}, to_apply=%all_to_all.3.reduce_sub_computation | reduce | bytes 2097156 | tf_op jit(solution)/shard_map/all_to_all | solution.py:199
  61.3 1.4 %reshape.598 = f32[256,2,2,1,4,64]{5,4,3,2,1,0:T(4,128)S(1)} reshape(f32[256,1024]{1,0:T(8,128)S(1)} %reduce) | data formatting | bytes 2097152
  62.7 1.2 copy.55
  64.0 1.1 copy.56
  65.1 1.8 %copy.89 = f32[2,4,1,4,128,64]{5,4,0,3,1,2:T(8,128)S(1)} copy(f32[2,4,1,4,128,64]{4,5,3,2,1,0:T(8,128)} %bitcast.183) | data formatting | bytes 2097152 | tf_op jit(solution)/shard_map/reshape
  66.9 0.3 reshape.584
  67.3 2.0 %convolution_bitcast_fusion.4 = f32[2,4,1,4,64,128]{5,4,0,3,1,2:T(8,128)S(1)} fusion(f32[2,4,4,64,128,1]{4,3,0,2,1,5:T(8,128)S(1)} %reshape.584, f32[1,2,64,64]{3,2,1,0:T(8,128)} %get-tuple-element.25, f32[1,2,64,64]{3,2,1,0:T(8,128)} %get-tuple-element.24), kind=kOutput, calls=%fused_computation.7 | convolution fusion | flops 402669568 | bytes 2162688 | tf_op jit(solution)/shard_map/pqkn,q...nm->p...km/dot_general | solution.py:252
  69.3 0.9 multiply_subtract_fusion.2
  70.3 1.0 convolution_bitcast_fusion.3
  71.4 0.2 multiply_subtract_fusion.1
  71.6 1.0 convolution_bitcast_fusion.2
  72.6 0.2 multiply_subtract_fusion
  72.8 1.1 fusion.1
  73.9 0.6 reshape.596
  74.5 0.7 copy_multiply_fusion
  75.2 0.5 fusion.66
  75.7 0.5 copy.62
  76.2 6.9 %collective-permute-start = (f32[2,4,3,8192]{3,1,2,0:T(4,128)S(1)}, f32[2,4,3,8192]{3,1,2,0:T(4,128)S(1)}, u32[]{:S(2)}, u32[]{:S(2)}) collective-permute-start(f32[2,4,3,8192]{3,1,2,0:T(4,128)S(1)} %copy.62), channel_id=1, source_target_pairs={{0,1},{1,2},{2,3},{3,4},{4,5},{5,6},{6,7},{7,8},{8,9},{9,10},{10,1... | collective-permute-start | bytes 2359304 | tf_op jit(solution)/shard_map/ppermute | solution.py:212
  83.1 0.5 copy.63
  83.7 1.9 %collective-permute-start.1 = (f32[2,4,3,8192]{3,1,2,0:T(4,128)S(1)}, f32[2,4,3,8192]{3,1,2,0:T(4,128)}, u32[]{:S(2)}, u32[]{:S(2)}) collective-permute-start(f32[2,4,3,8192]{3,1,2,0:T(4,128)S(1)} %copy.63), channel_id=1, source_target_pairs={{1,0},{2,1},{3,2},{4,3},{5,4},{6,5},{7,6},{8,7},{9,8},{10,9},{11,1... | collective-permute-start | bytes 2359304 | tf_op jit(solution)/shard_map/ppermute | solution.py:213
  85.6 0.1 pad.3.clone
  85.7 0.8 fusion.18.band_ref
  86.4 5.6 %collective-permute-done = f32[2,4,3,8192]{3,1,2,0:T(4,128)S(1)} collective-permute-done((f32[2,4,3,8192]{3,1,2,0:T(4,128)S(1)}, f32[2,4,3,8192]{3,1,2,0:T(4,128)S(1)}, u32[]{:S(2)}, u32[]{:S(2)}) %collective-permute-start) | collective-permute-done | bytes 786464 | tf_op jit(solution)/shard_map/ppermute | solution.py:212
  92.1 0.5 copy.64
  92.6 8.7 %collective-permute-done.1 = f32[2,4,3,8192]{3,1,2,0:T(4,128)} collective-permute-done((f32[2,4,3,8192]{3,1,2,0:T(4,128)S(1)}, f32[2,4,3,8192]{3,1,2,0:T(4,128)}, u32[]{:S(2)}, u32[]{:S(2)}) %collective-permute-start.1) | collective-permute-done | bytes 786464 | tf_op jit(solution)/shard_map/ppermute | solution.py:213
  101.3 1.7 %copy.65 = f32[2,4,3,8192]{3,2,1,0:T(4,128)S(1)} copy(f32[2,4,3,8192]{3,1,2,0:T(4,128)} %collective-permute-done.1) | data formatting | bytes 1572864 | tf_op jit(solution)/shard_map/ppermute | solution.py:213
  103.0 3.1 %maximum_maximum_fusion.prev_ref.cur_ref.next_ref = f32[2,4,16,8192]{3,2,1,0:T(8,128)} fusion(f32[2,4,3,8192]{3,2,1,0:T(4,128)S(1)} %copy.65, f32[2,4,4,8192]{3,2,1,0:T(4,128)S(1)} %copy_multiply_fusion, f32[2,4,3,8192]{3,2,1,0:T(4,128)S(1)} %copy.64, f32[16]{0:T(128)S(1)} %pad.3.clone), kind=kLoop, calls=%fused_computation | loop fusion | flops 3145728 | bytes 6815808 | tf_op jit(solution)/shard_map/concatenate | solution.py:141
  106.0 0.7 broadcast_in_dim.4.mask_ref
  106.7 20.5 %shard_map.59 = (f32[2,4,4,8192]{3,2,1,0:T(4,128)}, f32[4,8192]{1,0:T(4,128)}) custom-call(f32[8,128]{1,0:T(8,128)} %broadcast_in_dim.4.mask_ref, bf16[384,128]{1,0:T(8,128)(2,1)} %fusion.18.band_ref, f32[2,4,16,8192]{3,2,1,0:T(8,128)} %maximum_maximum_fusion.prev_ref.cur_ref.next_ref, f32[2,4,16,8192]{3,2,1,0:T(8,128)} %maximum_maximum_fusion.prev_ref.cur_ref.next_ref, ...), custom_call_target="tpu_custom_call" | custom-call | tf_op jit(solution)/shard_map/pallas_call | solution.py:153
  (36 shorter events, 0.6 us)
Async XLA Ops:
  6.2 1.2 copy-start
  12.7 17.6 %copy-start.8 = (f32[8192]{0:T(1024)S(1)}, f32[8192]{0:T(1024)}, u32[]{:S(2)}) copy-start(f32[8192]{0:T(1024)} %param.6) | copy-start | bytes 98308
  15.6 42.1 %all-to-all-start = ((f32[256,1,1024]{2,1,0:T(1,128)}), f32[256,1,1024]{2,1,0:T(1,128)S(1)}, u32[]{:S(2)}, u32[]{:S(2)}) async-start(f32[256,1,1024]{2,1,0:T(1,128)} %reshape.597), calls=%async_computation | async-start | bytes 2097152 | tf_op jit(solution)/shard_map/all_to_all | solution.py:199
  67.3 4.1 %copy-start.4 = (f32[64,128]{1,0:T(8,128)S(1)}, f32[64,128]{1,0:T(8,128)}, u32[]{:S(2)}) copy-start(f32[64,128]{1,0:T(8,128)} %copy.59) | copy-start | bytes 98308
  67.3 4.1 %copy-start.5 = (f32[64,128]{1,0:T(8,128)S(1)}, f32[64,128]{1,0:T(8,128)}, u32[]{:S(2)}) copy-start(f32[64,128]{1,0:T(8,128)} %copy.60) | copy-start | bytes 98308
  67.3 4.2 %copy-start.1 = (f32[1,2,128,128]{3,2,1,0:T(8,128)S(1)}, f32[1,2,128,128]{3,2,1,0:T(8,128)}, u32[]{:S(2)}) copy-start(f32[1,2,128,128]{3,2,1,0:T(8,128)} %copy-done) | copy-start | bytes 393220
  69.3 3.3 %copy-start.6 = (f32[64,128]{1,0:T(8,128)S(1)}, f32[64,128]{1,0:T(8,128)}, u32[]{:S(2)}) copy-start(f32[64,128]{1,0:T(8,128)} %get-tuple-element.48) | copy-start | bytes 98308
  69.3 3.3 %copy-start.7 = (f32[64,128]{1,0:T(8,128)S(1)}, f32[64,128]{1,0:T(8,128)}, u32[]{:S(2)}) copy-start(f32[64,128]{1,0:T(8,128)} %get-tuple-element.49) | copy-start | bytes 98308
  70.3 2.5 %copy-start.2 = (f32[1,2,64,64]{3,2,1,0:T(8,128)S(1)}, f32[1,2,64,64]{3,2,1,0:T(8,128)}, u32[]{:S(2)}) copy-start(f32[1,2,64,64]{3,2,1,0:T(8,128)} %get-tuple-element.20) | copy-start | bytes 98308
  70.3 2.5 %copy-start.3 = (f32[1,2,64,64]{3,2,1,0:T(8,128)S(1)}, f32[1,2,64,64]{3,2,1,0:T(8,128)}, u32[]{:S(2)}) copy-start(f32[1,2,64,64]{3,2,1,0:T(8,128)} %get-tuple-element.21) | copy-start | bytes 98308
  71.5 3.0 %copy-start.9 = (f32[4,4]{1,0:T(4,128)S(1)}, f32[4,4]{1,0:T(4,128)}, u32[]{:S(2)}) copy-start(f32[4,4]{1,0:T(4,128)} %param.7) | copy-start | bytes 196
  76.2 15.8 %collective-permute-start = (f32[2,4,3,8192]{3,1,2,0:T(4,128)S(1)}, f32[2,4,3,8192]{3,1,2,0:T(4,128)S(1)}, u32[]{:S(2)}, u32[]{:S(2)}) collective-permute-start(f32[2,4,3,8192]{3,1,2,0:T(4,128)S(1)} %copy.62), channel_id=1, source_target_pairs={{0,1},{1,2},{2,3},{3,4},{4,5},{5,6},{6,7},{7,8},{8,9},{9,10},{10,1... | collective-permute-start | bytes 2359304 | tf_op jit(solution)/shard_map/ppermute | solution.py:212
  83.7 17.6 %collective-permute-start.1 = (f32[2,4,3,8192]{3,1,2,0:T(4,128)S(1)}, f32[2,4,3,8192]{3,1,2,0:T(4,128)}, u32[]{:S(2)}, u32[]{:S(2)}) collective-permute-start(f32[2,4,3,8192]{3,1,2,0:T(4,128)S(1)} %copy.63), channel_id=1, source_target_pairs={{1,0},{2,1},{3,2},{4,3},{5,4},{6,5},{7,6},{8,7},{9,8},{10,9},{11,1... | collective-permute-start | bytes 2359304 | tf_op jit(solution)/shard_map/ppermute | solution.py:213

commit v2 on v1

--- a/solution.py
+++ b/solution.py
@@ -19,15 +19,24 @@
 ROWS = 8
 
 
-def link_kernel(mask_ref, band_ref, prev_ref, cur_ref, next_ref, vec_ref, qual_ref, image, terms, high, low, sums):
+def link_kernel(mask_ref, band_ref, *refs):
+    pieces = refs[:9]
+    vec_ref, qual_ref, image, terms, high, low, sums = refs[9:]
     step = pl.program_id(0)
     last = pl.num_programs(0) - 1
-    dates = cur_ref.shape[1]
-    block = cur_ref.shape[3]
-    padded = cur_ref.shape[2]
-    image[:, :, :, EDGE : EDGE + block] = cur_ref[...]
-    image[:, :, :, :EDGE] = jnp.where(step > 0, prev_ref[...], 0.0)
-    image[:, :, :, EDGE + block :] = jnp.where(step < last, next_ref[...], 0.0)
+    dates = pieces[1].shape[1]
+    block = pieces[1].shape[3]
+    padded = image.shape[2]
+    row = 0
+    for number in range(3):
+        prev_ref, cur_ref, next_ref = pieces[3 * number : 3 * number + 3]
+        count = cur_ref.shape[2]
+        rows = slice(row, row + count)
+        image[:, :, rows, EDGE : EDGE + block] = cur_ref[...]
+        image[:, :, rows, :EDGE] = jnp.where(step > 0, prev_ref[...], 0.0)
+        image[:, :, rows, EDGE + block :] = jnp.where(step < last, next_ref[...], 0.0)
+        row += count
+    image[:, :, row:, :] = jnp.zeros((image.shape[0], dates, padded - row, image.shape[3]), jnp.float32)
     pairs = [(a, b) for a in range(dates) for b in range(a + 1, dates)]
     specs = [(0, a, a) for a in range(dates)]
     for a, b in pairs:
@@ -135,12 +144,9 @@
     lax.fori_loop(0, block // CHUNK, chunk_body, 0)
 
 
-def link_and_smooth(extended, valid_mask):
-    parts, dates, columns, lines = extended.shape
+def link_and_smooth(pieces, valid_mask):
+    parts, dates, _, lines = pieces[1].shape
     padded = 16
-    extended = jnp.concatenate(
-        [extended, jnp.zeros((parts, dates, padded - columns, lines), extended.dtype)], axis=2
-    )
     kept = ROWS - 2 * SMOOTH_PASSES
     steps = lines // BLOCK
     per_block = BLOCK // EDGE
@@ -150,16 +156,24 @@
     offset = jnp.arange(CHUNK + 2 * EDGE, dtype=jnp.int32)[:, None] - EDGE - jnp.arange(CHUNK, dtype=jnp.int32)[None, :]
     band = (jnp.abs(offset) <= WIN_HALF).astype(jnp.bfloat16)
     width = BLOCK + 2 * EDGE
+    piece_specs = []
+    operands = []
+    for piece in pieces:
+        count = piece.shape[2]
+        piece_specs += [
+            pl.BlockSpec((parts, dates, count, EDGE), lambda i: (0, 0, 0, jnp.maximum(i * per_block - 1, 0))),
+            pl.BlockSpec((parts, dates, count, BLOCK), lambda i: (0, 0, 0, i)),
+            pl.BlockSpec((parts, dates, count, EDGE), lambda i: (0, 0, 0, jnp.minimum((i + 1) * per_block, edges - 1))),
+        ]
+        operands += [piece, piece, piece]
     return pl.pallas_call(
         link_kernel,
         grid=(steps,),
         in_specs=[
             pl.BlockSpec((ROWS, CHUNK), lambda i: (0, 0)),
             pl.BlockSpec((CHUNK + 2 * EDGE, CHUNK), lambda i: (0, 0)),
-            pl.BlockSpec((parts, dates, padded, EDGE), lambda i: (0, 0, 0, jnp.maximum(i * per_block - 1, 0))),
-            pl.BlockSpec((parts, dates, padded, BLOCK), lambda i: (0, 0, 0, i)),
-            pl.BlockSpec((parts, dates, padded, EDGE), lambda i: (0, 0, 0, jnp.minimum((i + 1) * per_block, edges - 1))),
-        ],
+        ]
+        + piece_specs,
         out_specs=[
             pl.BlockSpec((parts, dates, kept, BLOCK), lambda i: (0, 0, 0, i)),
             pl.BlockSpec((kept, BLOCK), lambda i: (0, i)),
@@ -175,7 +189,7 @@
             pltpu.VMEM((term_count * ROWS, width), jnp.bfloat16),
             pltpu.VMEM((term_count * ROWS, BLOCK), jnp.float32),
         ],
-    )(mask, band, extended, extended, extended)
+    )(mask, band, *operands)
 
 
 def split_up(x, dim, count):
@@ -280,6 +294,15 @@
     inverse_rows = dft_table(outer_size, 1)
     result = jnp.einsum("pqnk,qdlkm->pdnml", inverse_rows, spectrum, precision=HIGHEST) / length
     return result.reshape(2, values.shape[1], row_count * inner_size, values.shape[2])
+
+
+def range_blocks(values, phases):
+    length = values.shape[-1]
+    inner_size = 128
+    outer_size = length // inner_size
+    spectrum = spectral_core(values.reshape(values.shape[:-1] + (outer_size, inner_size)), phases)
+    inverse_rows = dft_table(outer_size, 1)
+    return jnp.einsum("pqnk,qdlkm->nmpdl", inverse_rows, spectrum, precision=HIGHEST) / length
 
 
 def running_window(values):
@@ -376,21 +399,32 @@
     local_lines = raw_echoes.shape[2]
     length = raw_echoes.shape[3]
     outer_size = length // 128
-    ranged = range_compress(raw_echoes.astype(jnp.float32), range_phase, outer_size)
-    ranged = ranged.reshape(2, group_dates, groups, length // groups, local_lines)
-    turned = one_exchange(ranged, ("date", "strip"), ("date", "strip"), (2, 3), (1, 4))
+    devices = groups * lax.axis_size("strip")
+    ranged = range_blocks(raw_echoes.astype(jnp.float32), range_phase)
+    tiles = ranged.reshape(devices, -1, 128)
+    tiles = lax.all_to_all(tiles, ("date", "strip"), 0, 0, tiled=True)
+    strips = devices // groups
+    block_range = length // devices
+    received = tiles.reshape(groups, strips, block_range, 2, group_dates, local_lines)
+    turned = received.transpose(3, 0, 4, 2, 1, 5).reshape(
+        2, groups * group_dates, block_range, strips * local_lines
+    )
     focused = azimuth_compress(turned, azimuth_phase)
     all_dates = group_dates * groups
     column_count = calibration.shape[1]
     line_count = focused.shape[-1]
     image = focused.reshape(2, all_dates, column_count, line_count) * calibration[None, :, :, None]
     halo = 1 + SMOOTH_PASSES
-    extended = extended_2(image, ((("date", "strip"), 2),), halo)
+    axes = ("date", "strip")
+    count = lax.axis_size("date") * lax.axis_size("strip")
+    up = [(i, i + 1) for i in range(count - 1)]
+    low = lax.ppermute(image[:, :, column_count - halo :], axes, up)
+    high = lax.ppermute(image[:, :, :halo], axes, [(b, a) for a, b in up])
     total_columns = column_count * lax.axis_size("date") * lax.axis_size("strip")
     first = lax.axis_index(("date", "strip")) * column_count - SMOOTH_PASSES
     columns = first + jnp.arange(column_count + 2 * SMOOTH_PASSES, dtype=jnp.int32)
     valid_mask = ((columns >= 0) & (columns < total_columns)).astype(jnp.float32)
-    vector, quality = link_and_smooth(extended, valid_mask)
+    vector, quality = link_and_smooth((low, image, high), valid_mask)
     return (vector, quality)
 
 

time: 128 us -> 114 us (0.89)
  other arithmetic: 14.2 us -> 7.16 us
  local copies, waits for them, and re-layouts: 22.4 us -> 15.6 us
    unnamed x23 -> x27, local copies, waits for them, and re-layouts: 5.47 us -> 1.66 us
    all_to_all x1 -> x0, other arithmetic: 3.13 us -> none  [one_exchange(): tiles = lax.all_to_all(tiles, axis, split_axis=0, concat_axis=0, tiled=True)]
    concatenate x1 -> x0, other arithmetic: 3.06 us -> none  [link_and_smooth(): jnp.concatenate([extended, jnp.zeros((parts, dates, padded - columns, lin...]
    another operation x4 -> x2, local copies, waits for them, and re-layouts: 2.93 us -> 1.14 us  [azimuth_compress(): values.reshape(values.shape[:-1] + (outer_size, inner_size))]
    all_to_all x2 -> x1, local copies, waits for them, and re-layouts: 1.76 us -> 0.39 us  [shards(): tiles = lax.all_to_all(tiles, ('date', 'strip'), 0, 0, tiled=True)]
    div x0 -> x1, local copies, waits for them, and re-layouts: none -> 1.3 us  [range_blocks(): jnp.einsum('pqnk,qdlkm->nmpdl', inverse_rows, spectrum, precision=HIGHEST)]
  transfers between devices with their start and end apart: 3 -> 3, of which waited for: 3 -> 3; matrix products, arithmetic and copies ran while one was open for 6% -> 7% of each run, Pallas kernels for 0% -> 0%
where the time goes in v2:
time: 114 us
  waiting for transfers between devices  35.6 us (31%)
  starting transfers between devices  23.5 us (21%)
  Pallas kernels  21.7 us (19%)
  local copies, waits for them, and re-layouts  15.6 us (14%)
  matrix products  8.83 us (8%)
  other arithmetic  7.16 us (6%)
  between operations  1.33 us (1%)
    all_to_all x1, waiting for transfers between devices, shards(): tiles = lax.all_to_all(tiles, ('date', 'strip'), 0, 0, tiled=True)  22.3 us
    pallas_call x1, Pallas kernels, link_and_smooth(): pl.pallas_call(link_kernel, grid=(steps,), in_specs=[pl.BlockSpec((ROWS,...  21.7 us
    all_to_all x1, starting transfers between devices, shards(): tiles = lax.all_to_all(tiles, ('date', 'strip'), 0, 0, tiled=True)  14.7 us
    ppermute x1, waiting for transfers between devices, shards(): high = lax.ppermute(image[:, :, :halo], axes, [(b, a) for a, b in up])  7.6 us
    ppermute x1, starting transfers between devices, shards(): low = lax.ppermute(image[:, :, column_count - halo:], axes, up)  6.9 us
    ppermute x1, waiting for transfers between devices, shards(): low = lax.ppermute(image[:, :, column_count - halo:], axes, up)  5.68 us
    dot_general x2, matrix products, spectral_core(): jnp.einsum('pqkn,q...nm->p...km', dft_table(outer_size, -1), values, prec...  2.62 us
  transfers between devices with their start and end apart: 3, of which 3 were waited for; matrix products, arithmetic and copies ran while one was open for 7% of the time, Pallas kernels for 0%

profile of v2, /device:TPU:31, one launch (start us, length us, event | category | flops | bytes accessed | tf_op | source)
XLA Modules:
  0.0 113.7 jit_solution(1960075075052408180)
XLA Ops:
  0.6 0.1 fusion.57
  0.7 0.1 fusion.56
  0.7 0.1 multiply_sine_fusion.9
  0.8 0.1 multiply_sine_fusion.8
  0.8 0.1 multiply_sine_fusion.7
  0.9 0.1 multiply_sine_fusion.6
  1.0 0.3 fusion.39
  1.2 0.3 fusion.38
  1.5 0.3 multiply_sine_fusion.1
  1.8 0.3 multiply_sine_fusion
  2.1 0.7 fusion.68
  2.8 0.1 cos.132
  2.9 0.1 sin.156
  3.1 1.2 %copy.65 = bf16[32,8,8,128]{3,2,1,0:T(8,128)(2,1)S(1)} copy(bf16[32,8,8,128]{3,1,2,0:T(8,128)(2,1)} %bitcast.161) | data formatting | bytes 1048576
  4.3 0.6 convolution_bitcast_fusion
  5.0 0.1 multiply_subtract_fusion.5
  5.1 1.0 convolution_bitcast_fusion.7
  6.1 0.1 multiply_subtract_fusion.4
  6.3 1.0 convolution_bitcast_fusion.6
  7.3 0.1 multiply_subtract_fusion.3
  7.4 1.0 fusion.3
  8.4 1.3 %copy.24 = f32[8,128,2,2,64]{4,3,2,1,0:T(2,128)S(1)} copy(f32[8,128,2,2,64]{1,0,2,4,3:T(8,128)S(1)} %fusion.3) | data formatting | bytes 2097152 | tf_op jit(solution)/shard_map/div | solution.py:305
  9.8 2.1 %reshape.488 = f32[256,8,128]{2,1,0:T(8,128)} reshape(f32[8,128,2,2,64]{4,3,2,1,0:T(2,128)S(1)} %copy.24) | data formatting | bytes 2097152 | tf_op jit(solution)/shard_map/reshape | solution.py:404
  11.9 14.7 %all-to-all-start = ((f32[256,8,128]{2,1,0:T(8,128)}), f32[256,8,128]{2,1,0:T(8,128)S(1)}, u32[]{:S(2)}, u32[]{:S(2)}) async-start(f32[256,8,128]{2,1,0:T(8,128)} %reshape.488), calls=%async_computation | async-start | bytes 2097152 | tf_op jit(solution)/shard_map/all_to_all | solution.py:405
  26.6 0.1 fusion.67
  26.7 0.1 cos.140
  26.8 0.7 copy.28
  27.5 0.1 sin.164
  27.6 0.7 copy.29
  28.3 0.1 fusion.45
  28.4 0.1 fusion.44
  28.6 0.1 multiply_sine_fusion.5
  28.7 0.8 multiply_sine_fusion.4
  29.5 0.8 multiply_sine_fusion.3
  30.2 0.1 multiply_sine_fusion.2
  30.4 0.7 maximum_bitcast_fusion.25
  31.1 0.7 maximum_bitcast_fusion.27
  31.7 22.3 %all-to-all-done = f32[256,8,128]{2,1,0:T(8,128)S(1)} async-done(((f32[256,8,128]{2,1,0:T(8,128)}), f32[256,8,128]{2,1,0:T(8,128)S(1)}, u32[]{:S(2)}, u32[]{:S(2)}) %all-to-all-start) | async-done | bytes 1048608 | tf_op jit(solution)/shard_map/all_to_all | solution.py:405
  54.0 0.4 copy.25
  54.4 0.5 reshape.489
  55.0 0.8 copy.62
  55.8 0.3 reshape.503
  56.1 2.0 %convolution_bitcast_fusion.4 = f32[2,4,4,64,128]{4,3,0,2,1:T(8,128)S(1)} fusion(f32[2,4,4,64,128,1]{4,3,0,2,1,5:T(8,128)S(1)} %reshape.503, f32[1,2,64,64]{3,2,1,0:T(8,128)} %get-tuple-element.25, f32[1,2,64,64]{3,2,1,0:T(8,128)} %get-tuple-element.24), kind=kOutput, calls=%fused_computation.6 | convolution fusion | flops 402669568 | bytes 2162688 | tf_op jit(solution)/shard_map/pqkn,q...nm->p...km/dot_general | solution.py:266
  58.2 0.2 multiply_subtract_fusion.2
  58.4 1.0 convolution_bitcast_fusion.3
  59.4 0.2 multiply_subtract_fusion.1
  59.6 1.0 convolution_bitcast_fusion.2
  60.7 0.2 multiply_subtract_fusion
  60.9 1.1 fusion.1
  62.0 0.6 reshape.515
  62.6 0.7 copy_multiply_fusion.refs_3_.refs_4_.refs_5_
  63.3 0.5 fusion.66
  63.8 0.4 copy-done
  64.3 0.5 copy.31
  64.8 6.9 %collective-permute-start = (f32[2,4,3,8192]{3,1,2,0:T(4,128)S(1)}, f32[2,4,3,8192]{3,1,2,0:T(4,128)S(1)}, u32[]{:S(2)}, u32[]{:S(2)}) collective-permute-start(f32[2,4,3,8192]{3,1,2,0:T(4,128)S(1)} %copy.31), channel_id=1, source_target_pairs={{0,1},{1,2},{2,3},{3,4},{4,5},{5,6},{6,7},{7,8},{8,9},{9,10},{10,1... | collective-permute-start | bytes 2359304 | tf_op jit(solution)/shard_map/ppermute | solution.py:421
  71.7 0.5 copy.32
  72.2 1.9 %collective-permute-start.1 = (f32[2,4,3,8192]{3,1,2,0:T(4,128)S(1)}, f32[2,4,3,8192]{3,1,2,0:T(4,128)S(1)}, u32[]{:S(2)}, u32[]{:S(2)}) collective-permute-start(f32[2,4,3,8192]{3,1,2,0:T(4,128)S(1)} %copy.32), channel_id=1, source_target_pairs={{1,0},{2,1},{3,2},{4,3},{5,4},{6,5},{7,6},{8,7},{9,8},{10,9},{11,1... | collective-permute-start | bytes 2359304 | tf_op jit(solution)/shard_map/ppermute | solution.py:422
  74.2 0.8 fusion.18.band_ref
  74.9 5.7 %collective-permute-done = f32[2,4,3,8192]{3,1,2,0:T(4,128)S(1)} collective-permute-done((f32[2,4,3,8192]{3,1,2,0:T(4,128)S(1)}, f32[2,4,3,8192]{3,1,2,0:T(4,128)S(1)}, u32[]{:S(2)}, u32[]{:S(2)}) %collective-permute-start) | collective-permute-done | bytes 786464 | tf_op jit(solution)/shard_map/ppermute | solution.py:421
  80.6 1.5 %copy.33.refs_0_.refs_1_.refs_2_ = f32[2,4,3,8192]{3,2,1,0:T(4,128)} copy(f32[2,4,3,8192]{3,1,2,0:T(4,128)S(1)} %collective-permute-done) | data formatting | bytes 1572864 | tf_op jit(solution)/shard_map/ppermute | solution.py:421
  82.1 7.6 %collective-permute-done.1 = f32[2,4,3,8192]{3,1,2,0:T(4,128)S(1)} collective-permute-done((f32[2,4,3,8192]{3,1,2,0:T(4,128)S(1)}, f32[2,4,3,8192]{3,1,2,0:T(4,128)S(1)}, u32[]{:S(2)}, u32[]{:S(2)}) %collective-permute-start.1) | collective-permute-done | bytes 786464 | tf_op jit(solution)/shard_map/ppermute | solution.py:422
  89.7 1.5 %copy.36.refs_6_.refs_7_.refs_8_ = f32[2,4,3,8192]{3,2,1,0:T(4,128)} copy(f32[2,4,3,8192]{3,1,2,0:T(4,128)S(1)} %collective-permute-done.1) | data formatting | bytes 1572864 | tf_op jit(solution)/shard_map/ppermute | solution.py:422
  91.3 0.6 broadcast_in_dim.2.mask_ref
  91.9 21.7 %shard_map.59 = (f32[2,4,4,8192]{3,2,1,0:T(4,128)}, f32[4,8192]{1,0:T(4,128)}) custom-call(f32[8,128]{1,0:T(8,128)} %broadcast_in_dim.2.mask_ref, bf16[384,128]{1,0:T(8,128)(2,1)} %fusion.18.band_ref, f32[2,4,3,8192]{3,2,1,0:T(4,128)} %copy.33.refs_0_.refs_1_.refs_2_, f32[2,4,3,8192]{3,2,1,0:T(4,128)} %copy.33.refs_0_.refs_1_.refs_2_, ...), custom_call_target="tpu_custom_call" | custom-call | tf_op jit(solution)/shard_map/pallas_call | solution.py:169
  (33 shorter events, 0.2 us)
Async XLA Ops:
  4.3 1.8 %copy-start.1 = (f32[1,2,128,128]{3,2,1,0:T(8,128)}, f32[1,2,128,128]{3,2,1,0:T(8,128)S(1)}, u32[]{:S(2)}) copy-start(f32[1,2,128,128]{3,2,1,0:T(8,128)S(1)} %get-tuple-element.19) | copy-start | bytes 393220
  9.7 16.8 %copy-start.11 = (f32[8192]{0:T(1024)S(1)}, f32[8192]{0:T(1024)}, u32[]{:S(2)}) copy-start(f32[8192]{0:T(1024)} %param.6) | copy-start | bytes 98308
  11.9 42.1 %all-to-all-start = ((f32[256,8,128]{2,1,0:T(8,128)}), f32[256,8,128]{2,1,0:T(8,128)S(1)}, u32[]{:S(2)}, u32[]{:S(2)}) async-start(f32[256,8,128]{2,1,0:T(8,128)} %reshape.488), calls=%async_computation | async-start | bytes 2097152 | tf_op jit(solution)/shard_map/all_to_all | solution.py:405
  56.1 2.0 %copy-start.9 = (f32[64,128]{1,0:T(8,128)S(1)}, f32[64,128]{1,0:T(8,128)}, u32[]{:S(2)}) copy-start(f32[64,128]{1,0:T(8,128)} %get-tuple-element.46) | copy-start | bytes 98308
  56.1 2.0 %copy-start.10 = (f32[64,128]{1,0:T(8,128)S(1)}, f32[64,128]{1,0:T(8,128)}, u32[]{:S(2)}) copy-start(f32[64,128]{1,0:T(8,128)} %get-tuple-element.47) | copy-start | bytes 98308
  56.1 2.2 %copy-start.2 = (f32[1,2,128,128]{3,2,1,0:T(8,128)S(1)}, f32[1,2,128,128]{3,2,1,0:T(8,128)}, u32[]{:S(2)}) copy-start(f32[1,2,128,128]{3,2,1,0:T(8,128)} %copy-done.1) | copy-start | bytes 393220
  58.2 1.2 %copy-start.5 = (f32[64,128]{1,0:T(8,128)S(1)}, f32[64,128]{1,0:T(8,128)}, u32[]{:S(2)}) copy-start(f32[64,128]{1,0:T(8,128)} %copy.28) | copy-start | bytes 98308
  58.2 1.2 %copy-start.6 = (f32[64,128]{1,0:T(8,128)S(1)}, f32[64,128]{1,0:T(8,128)}, u32[]{:S(2)}) copy-start(f32[64,128]{1,0:T(8,128)} %copy.29) | copy-start | bytes 98308
  59.4 1.2 %copy-start.7 = (f32[64,128]{1,0:T(8,128)S(1)}, f32[64,128]{1,0:T(8,128)}, u32[]{:S(2)}) copy-start(f32[64,128]{1,0:T(8,128)} %get-tuple-element.48) | copy-start | bytes 98308
  59.4 1.2 %copy-start.8 = (f32[64,128]{1,0:T(8,128)S(1)}, f32[64,128]{1,0:T(8,128)}, u32[]{:S(2)}) copy-start(f32[64,128]{1,0:T(8,128)} %get-tuple-element.49) | copy-start | bytes 98308
  59.6 1.2 %copy-start.3 = (f32[1,2,64,64]{3,2,1,0:T(8,128)S(1)}, f32[1,2,64,64]{3,2,1,0:T(8,128)}, u32[]{:S(2)}) copy-start(f32[1,2,64,64]{3,2,1,0:T(8,128)} %get-tuple-element.20) | copy-start | bytes 98308
  59.6 1.2 %copy-start.4 = (f32[1,2,64,64]{3,2,1,0:T(8,128)S(1)}, f32[1,2,64,64]{3,2,1,0:T(8,128)}, u32[]{:S(2)}) copy-start(f32[1,2,64,64]{3,2,1,0:T(8,128)} %get-tuple-element.21) | copy-start | bytes 98308
  60.9 1.7 %copy-start.12 = (f32[4,4]{1,0:T(4,128)S(1)}, f32[4,4]{1,0:T(4,128)}, u32[]{:S(2)}) copy-start(f32[4,4]{1,0:T(4,128)} %param.7) | copy-start | bytes 196
  63.3 1.0 copy-start
  64.8 15.8 %collective-permute-start = (f32[2,4,3,8192]{3,1,2,0:T(4,128)S(1)}, f32[2,4,3,8192]{3,1,2,0:T(4,128)S(1)}, u32[]{:S(2)}, u32[]{:S(2)}) collective-permute-start(f32[2,4,3,8192]{3,1,2,0:T(4,128)S(1)} %copy.31), channel_id=1, source_target_pairs={{0,1},{1,2},{2,3},{3,4},{4,5},{5,6},{6,7},{7,8},{8,9},{9,10},{10,1... | collective-permute-start | bytes 2359304 | tf_op jit(solution)/shard_map/ppermute | solution.py:421
  72.2 17.5 %collective-permute-start.1 = (f32[2,4,3,8192]{3,1,2,0:T(4,128)S(1)}, f32[2,4,3,8192]{3,1,2,0:T(4,128)S(1)}, u32[]{:S(2)}, u32[]{:S(2)}) collective-permute-start(f32[2,4,3,8192]{3,1,2,0:T(4,128)S(1)} %copy.32), channel_id=1, source_target_pairs={{1,0},{2,1},{3,2},{4,3},{5,4},{6,5},{7,6},{8,7},{9,8},{10,9},{11,1... | collective-permute-start | bytes 2359304 | tf_op jit(solution)/shard_map/ppermute | solution.py:422

commit v3 on v2

--- a/solution.py
+++ b/solution.py
@@ -1,4 +1,6 @@
 import math
+
+import numpy as np
 
 import jax
 import jax.numpy as jnp
@@ -24,17 +26,27 @@
     vec_ref, qual_ref, image, terms, high, low, sums = refs[9:]
     step = pl.program_id(0)
     last = pl.num_programs(0) - 1
-    dates = pieces[1].shape[1]
-    block = pieces[1].shape[3]
+    dates = pieces[4].shape[1]
+    block = pieces[4].shape[3]
     padded = image.shape[2]
     row = 0
     for number in range(3):
         prev_ref, cur_ref, next_ref = pieces[3 * number : 3 * number + 3]
-        count = cur_ref.shape[2]
-        rows = slice(row, row + count)
-        image[:, :, rows, EDGE : EDGE + block] = cur_ref[...]
-        image[:, :, rows, :EDGE] = jnp.where(step > 0, prev_ref[...], 0.0)
-        image[:, :, rows, EDGE + block :] = jnp.where(step < last, next_ref[...], 0.0)
+        if len(cur_ref.shape) == 4:
+            count = cur_ref.shape[2]
+            rows = slice(row, row + count)
+            image[:, :, rows, EDGE : EDGE + block] = cur_ref[...]
+            image[:, :, rows, :EDGE] = jnp.where(step > 0, prev_ref[...], 0.0)
+            image[:, :, rows, EDGE + block :] = jnp.where(step < last, next_ref[...], 0.0)
+        else:
+            count = cur_ref.shape[0] // (image.shape[0] * dates)
+            rows = slice(row, row + count)
+            for p in range(image.shape[0]):
+                for d in range(dates):
+                    source = slice((p * dates + d) * count, (p * dates + d + 1) * count)
+                    image[p, d, rows, EDGE : EDGE + block] = cur_ref[source, :]
+                    image[p, d, rows, :EDGE] = jnp.where(step > 0, prev_ref[source, :], 0.0)
+                    image[p, d, rows, EDGE + block :] = jnp.where(step < last, next_ref[source, :], 0.0)
         row += count
     image[:, :, row:, :] = jnp.zeros((image.shape[0], dates, padded - row, image.shape[3]), jnp.float32)
     pairs = [(a, b) for a in range(dates) for b in range(a + 1, dates)]
@@ -146,6 +158,7 @@
 
 def link_and_smooth(pieces, valid_mask):
     parts, dates, _, lines = pieces[1].shape
+    assert all(piece.shape[-1] == lines for piece in pieces)
     padded = 16
     kept = ROWS - 2 * SMOOTH_PASSES
     steps = lines // BLOCK
@@ -153,17 +166,17 @@
     edges = lines // EDGE
     term_count = dates + dates * (dates - 1)
     mask = jnp.broadcast_to(valid_mask[:, None], (ROWS, CHUNK))
-    offset = jnp.arange(CHUNK + 2 * EDGE, dtype=jnp.int32)[:, None] - EDGE - jnp.arange(CHUNK, dtype=jnp.int32)[None, :]
-    band = (jnp.abs(offset) <= WIN_HALF).astype(jnp.bfloat16)
+    offset = np.arange(CHUNK + 2 * EDGE)[:, None] - EDGE - np.arange(CHUNK)[None, :]
+    band = jnp.asarray(np.abs(offset) <= WIN_HALF, jnp.bfloat16)
     width = BLOCK + 2 * EDGE
     piece_specs = []
     operands = []
     for piece in pieces:
-        count = piece.shape[2]
+        lead = (0,) * (piece.ndim - 1)
         piece_specs += [
-            pl.BlockSpec((parts, dates, count, EDGE), lambda i: (0, 0, 0, jnp.maximum(i * per_block - 1, 0))),
-            pl.BlockSpec((parts, dates, count, BLOCK), lambda i: (0, 0, 0, i)),
-            pl.BlockSpec((parts, dates, count, EDGE), lambda i: (0, 0, 0, jnp.minimum((i + 1) * per_block, edges - 1))),
+            pl.BlockSpec(piece.shape[:-1] + (EDGE,), lambda i, lead=lead: lead + (jnp.maximum(i * per_block - 1, 0),)),
+            pl.BlockSpec(piece.shape[:-1] + (BLOCK,), lambda i, lead=lead: lead + (i,)),
+            pl.BlockSpec(piece.shape[:-1] + (EDGE,), lambda i, lead=lead: lead + (jnp.minimum((i + 1) * per_block, edges - 1),)),
         ]
         operands += [piece, piece, piece]
     return pl.pallas_call(
@@ -418,8 +431,9 @@
     axes = ("date", "strip")
     count = lax.axis_size("date") * lax.axis_size("strip")
     up = [(i, i + 1) for i in range(count - 1)]
-    low = lax.ppermute(image[:, :, column_count - halo :], axes, up)
-    high = lax.ppermute(image[:, :, :halo], axes, [(b, a) for a, b in up])
+    edge_shape = (-1, line_count)
+    low = lax.ppermute(image[:, :, column_count - halo :].reshape(edge_shape), axes, up)
+    high = lax.ppermute(image[:, :, :halo].reshape(edge_shape), axes, [(b, a) for a, b in up])
     total_columns = column_count * lax.axis_size("date") * lax.axis_size("strip")
     first = lax.axis_index(("date", "strip")) * column_count - SMOOTH_PASSES
     columns = first + jnp.arange(column_count + 2 * SMOOTH_PASSES, dtype=jnp.int32)

time: 114 us -> 114 us (level)
  waiting for transfers between devices: 35.6 us -> 37.9 us
  local copies, waits for them, and re-layouts: 15.6 us -> 13.5 us
    ppermute x2 -> x0, local copies, waits for them, and re-layouts: 3.06 us -> none  [the longest x1 1.53 us: shards(): low = lax.ppermute(image[:, :, column_count - halo:], axes, up)]
    ppermute x2, waiting for transfers between devices: 13.3 us -> 15.6 us  [the longest x1 8.7 us: shards(): lax.ppermute(image[:, :, :halo].reshape(edge_shape), axes, [(b, a) for a,...]
    reshape x0 -> x2, local copies, waits for them, and re-layouts: none -> 1.67 us  [the longest x1 1.27 us: shards(): image[:, :, column_count - halo:].reshape(edge_shape)]
  transfers between devices with their start and end apart: 3 -> 3, of which waited for: 3 -> 3; matrix products, arithmetic and copies ran while one was open for 7% -> 5% of each run, Pallas kernels for 0% -> 0%
where the time goes in v3:
time: 114 us; the launch traced here: 113 us
  waiting for transfers between devices  37.9 us (33%)
  starting transfers between devices  23.5 us (21%)
  Pallas kernels  21.9 us (19%)
  local copies, waits for them, and re-layouts  13.5 us (12%)
  matrix products  8.83 us (8%)
  other arithmetic  6.39 us (6%)
  between operations  1.31 us (1%)
    all_to_all x1, waiting for transfers between devices, shards(): tiles = lax.all_to_all(tiles, ('date', 'strip'), 0, 0, tiled=True)  22.3 us
    pallas_call x1, Pallas kernels, link_and_smooth(): pl.pallas_call(link_kernel, grid=(steps,), in_specs=[pl.BlockSpec((ROWS,...  21.9 us
    all_to_all x1, starting transfers between devices, shards(): tiles = lax.all_to_all(tiles, ('date', 'strip'), 0, 0, tiled=True)  14.7 us
    ppermute x1, waiting for transfers between devices, shards(): lax.ppermute(image[:, :, :halo].reshape(edge_shape), axes, [(b, a) for a,...  8.7 us
    ppermute x1, waiting for transfers between devices, shards(): lax.ppermute(image[:, :, column_count - halo:].reshape(edge_shape), axes,...  6.88 us
    ppermute x1, starting transfers between devices, shards(): lax.ppermute(image[:, :, column_count - halo:].reshape(edge_shape), axes,...  6.88 us
    dot_general x2, matrix products, spectral_core(): jnp.einsum('pqkn,q...nm->p...km', dft_table(outer_size, -1), values, prec...  2.62 us
  transfers between devices with their start and end apart: 3, of which 3 were waited for; matrix products, arithmetic and copies ran while one was open for 5% of the time, Pallas kernels for 0%

profile of v3, /device:TPU:31, one launch (start us, length us, event | category | flops | bytes accessed | tf_op | source)
XLA Modules:
  0.0 113.3 jit_solution(4221341278626574012)
XLA Ops:
  0.6 0.1 multiply_sine_fusion.9
  0.7 0.1 fusion.55
  0.7 0.1 multiply_sine_fusion.8
  0.8 0.3 multiply_sine_fusion.1
  1.1 0.3 fusion.37
  1.3 0.3 multiply_sine_fusion
  1.6 0.3 fusion.38
  1.9 0.1 multiply_sine_fusion.7
  1.9 0.1 multiply_sine_fusion.6
  2.0 0.1 fusion.56
  2.1 1.1 %copy.47 = bf16[32,8,8,128]{3,2,1,0:T(8,128)(2,1)S(1)} copy(bf16[32,8,8,128]{3,1,2,0:T(8,128)(2,1)} %bitcast.161) | data formatting | bytes 1048576
  3.2 0.7 fusion.67
  3.9 0.1 cos.132
  4.1 0.1 sin.156
  4.2 0.6 convolution_bitcast_fusion
  4.9 0.1 multiply_subtract_fusion.5
  5.0 1.0 convolution_bitcast_fusion.7
  6.1 0.1 multiply_subtract_fusion.4
  6.2 0.0 copy-start.3
  6.2 1.0 convolution_bitcast_fusion.6
  7.3 0.1 multiply_subtract_fusion.3
  7.4 1.0 fusion.3
  8.4 1.3 %copy.14 = f32[8,128,2,2,64]{4,3,2,1,0:T(2,128)S(1)} copy(f32[8,128,2,2,64]{1,0,2,4,3:T(8,128)S(1)} %fusion.3) | data formatting | bytes 2097152 | tf_op jit(solution)/shard_map/div | solution.py:318
  9.7 0.0 copy-start.13
  9.7 2.1 %reshape.489 = f32[256,8,128]{2,1,0:T(8,128)} reshape(f32[8,128,2,2,64]{4,3,2,1,0:T(2,128)S(1)} %copy.14) | data formatting | bytes 2097152 | tf_op jit(solution)/shard_map/reshape | solution.py:417
  11.9 14.7 %all-to-all-start = ((f32[256,8,128]{2,1,0:T(8,128)}), f32[256,8,128]{2,1,0:T(8,128)S(1)}, u32[]{:S(2)}, u32[]{:S(2)}) async-start(f32[256,8,128]{2,1,0:T(8,128)} %reshape.489), calls=%async_computation | async-start | bytes 2097152 | tf_op jit(solution)/shard_map/all_to_all | solution.py:418
  26.6 0.1 fusion.66
  26.7 0.1 cos.140
  26.8 0.7 copy.18
  27.5 0.1 sin.164
  27.6 0.7 copy.19
  28.3 0.1 fusion.43
  28.4 0.1 fusion.44
  28.5 0.1 multiply_sine_fusion.5
  28.7 0.8 multiply_sine_fusion.4
  29.5 0.8 multiply_sine_fusion.3
  30.2 0.1 multiply_sine_fusion.2
  30.4 0.7 maximum_bitcast_fusion.25
  31.0 0.7 maximum_bitcast_fusion.27
  31.7 22.3 %all-to-all-done = f32[256,8,128]{2,1,0:T(8,128)S(1)} async-done(((f32[256,8,128]{2,1,0:T(8,128)}), f32[256,8,128]{2,1,0:T(8,128)S(1)}, u32[]{:S(2)}, u32[]{:S(2)}) %all-to-all-start) | async-done | bytes 1048608 | tf_op jit(solution)/shard_map/all_to_all | solution.py:418
  54.0 0.4 copy.15
  54.4 0.5 reshape.490
  54.9 0.8 copy.44
  55.7 0.3 reshape.506
  56.1 2.0 %convolution_bitcast_fusion.4 = f32[2,4,4,64,128]{4,3,0,2,1:T(8,128)S(1)} fusion(f32[2,4,4,64,128,1]{4,3,0,2,1,5:T(8,128)S(1)} %reshape.506, f32[1,2,64,64]{3,2,1,0:T(8,128)} %get-tuple-element.25, f32[1,2,64,64]{3,2,1,0:T(8,128)} %get-tuple-element.24), kind=kOutput, calls=%fused_computation.6 | convolution fusion | flops 402669568 | bytes 2162688 | tf_op jit(solution)/shard_map/pqkn,q...nm->p...km/dot_general | solution.py:279
  58.1 0.2 multiply_subtract_fusion.2
  58.3 1.0 convolution_bitcast_fusion.3
  59.4 0.2 multiply_subtract_fusion.1
  59.6 1.0 convolution_bitcast_fusion.2
  60.7 0.2 multiply_subtract_fusion
  60.9 1.1 fusion.1
  62.0 0.6 reshape.518
  62.6 0.7 copy_multiply_fusion.refs_3_.refs_4_.refs_5_
  63.3 0.5 fusion.65
  63.8 0.5 copy-done
  64.3 1.3 %reshape.492 = f32[24,8192]{1,0:T(8,128)} reshape(f32[2,4,3,8192]{3,2,1,0:T(4,128)S(1)} %get-tuple-element.15) | data formatting | bytes 1572864 | tf_op jit(solution)/shard_map/reshape | solution.py:435
  65.5 6.9 %collective-permute-start = (f32[24,8192]{1,0:T(8,128)}, f32[24,8192]{1,0:T(8,128)S(1)}, u32[]{:S(2)}, u32[]{:S(2)}) collective-permute-start(f32[24,8192]{1,0:T(8,128)} %reshape.492), channel_id=1, source_target_pairs={{0,1},{1,2},{2,3},{3,4},{4,5},{5,6},{6,7},{7,8},{8,9},{9,10},{10,1... | collective-permute-start | bytes 2359304 | tf_op jit(solution)/shard_map/ppermute | solution.py:435
  72.4 0.4 reshape.493
  72.8 1.9 %collective-permute-start.1 = (f32[24,8192]{1,0:T(8,128)S(1)}, f32[24,8192]{1,0:T(8,128)S(1)}, u32[]{:S(2)}, u32[]{:S(2)}) collective-permute-start(f32[24,8192]{1,0:T(8,128)S(1)} %reshape.493), channel_id=1, source_target_pairs={{1,0},{2,1},{3,2},{4,3},{5,4},{6,5},{7,6},{8,7},{9,8},{10,9},{11,1... | collective-permute-start | bytes 2359304 | tf_op jit(solution)/shard_map/ppermute | solution.py:436
  74.8 6.9 %collective-permute-done.refs_0_.refs_1_.refs_2_ = f32[24,8192]{1,0:T(8,128)S(1)} collective-permute-done((f32[24,8192]{1,0:T(8,128)}, f32[24,8192]{1,0:T(8,128)S(1)}, u32[]{:S(2)}, u32[]{:S(2)}) %collective-permute-start) | collective-permute-done | bytes 786464 | tf_op jit(solution)/shard_map/ppermute | solution.py:435
  81.6 8.7 %collective-permute-done.1.refs_6_.refs_7_.refs_8_ = f32[24,8192]{1,0:T(8,128)S(1)} collective-permute-done((f32[24,8192]{1,0:T(8,128)S(1)}, f32[24,8192]{1,0:T(8,128)S(1)}, u32[]{:S(2)}, u32[]{:S(2)}) %collective-permute-start.1) | collective-permute-done | bytes 786464 | tf_op jit(solution)/shard_map/ppermute | solution.py:436
  90.3 0.8 broadcast_in_dim.2.mask_ref
  91.1 0.1 copy-done.2
  91.2 21.9 %shard_map.68 = (f32[2,4,4,8192]{3,2,1,0:T(4,128)}, f32[4,8192]{1,0:T(4,128)}) custom-call(f32[8,128]{1,0:T(8,128)} %broadcast_in_dim.2.mask_ref, bf16[384,128]{1,0:T(8,128)(2,1)} %constant.136.clone.band_ref, f32[24,8192]{1,0:T(8,128)} %copy-done.1, f32[24,8192]{1,0:T(8,128)} %copy-done.1, f32[24,8192]{1,0:T(8,128)} %copy-done.1, ...), custom_call_target="tpu_custom_call" | custom-call | tf_op jit(solution)/shard_map/pallas_call | solution.py:182
  (33 shorter events, 0.2 us)
Async XLA Ops:
  6.2 1.2 %copy-start.3 = (f32[1,2,128,128]{3,2,1,0:T(8,128)}, f32[1,2,128,128]{3,2,1,0:T(8,128)S(1)}, u32[]{:S(2)}) copy-start(f32[1,2,128,128]{3,2,1,0:T(8,128)S(1)} %get-tuple-element.17) | copy-start | bytes 393220
  9.7 16.8 %copy-start.13 = (f32[8192]{0:T(1024)S(1)}, f32[8192]{0:T(1024)}, u32[]{:S(2)}) copy-start(f32[8192]{0:T(1024)} %param.7) | copy-start | bytes 98308
  11.9 42.1 %all-to-all-start = ((f32[256,8,128]{2,1,0:T(8,128)}), f32[256,8,128]{2,1,0:T(8,128)S(1)}, u32[]{:S(2)}, u32[]{:S(2)}) async-start(f32[256,8,128]{2,1,0:T(8,128)} %reshape.489), calls=%async_computation | async-start | bytes 2097152 | tf_op jit(solution)/shard_map/all_to_all | solution.py:418
  56.1 2.0 %copy-start.11 = (f32[64,128]{1,0:T(8,128)S(1)}, f32[64,128]{1,0:T(8,128)}, u32[]{:S(2)}) copy-start(f32[64,128]{1,0:T(8,128)} %get-tuple-element.46) | copy-start | bytes 98308
  56.1 2.0 %copy-start.12 = (f32[64,128]{1,0:T(8,128)S(1)}, f32[64,128]{1,0:T(8,128)}, u32[]{:S(2)}) copy-start(f32[64,128]{1,0:T(8,128)} %get-tuple-element.47) | copy-start | bytes 98308
  58.1 1.2 %copy-start.7 = (f32[64,128]{1,0:T(8,128)S(1)}, f32[64,128]{1,0:T(8,128)}, u32[]{:S(2)}) copy-start(f32[64,128]{1,0:T(8,128)} %copy.18) | copy-start | bytes 98308
  58.1 1.2 %copy-start.8 = (f32[64,128]{1,0:T(8,128)S(1)}, f32[64,128]{1,0:T(8,128)}, u32[]{:S(2)}) copy-start(f32[64,128]{1,0:T(8,128)} %copy.19) | copy-start | bytes 98308
  58.3 1.3 %copy-start.4 = (f32[1,2,128,128]{3,2,1,0:T(8,128)S(1)}, f32[1,2,128,128]{3,2,1,0:T(8,128)}, u32[]{:S(2)}) copy-start(f32[1,2,128,128]{3,2,1,0:T(8,128)} %copy-done.3) | copy-start | bytes 393220
  59.4 1.3 %copy-start.9 = (f32[64,128]{1,0:T(8,128)S(1)}, f32[64,128]{1,0:T(8,128)}, u32[]{:S(2)}) copy-start(f32[64,128]{1,0:T(8,128)} %get-tuple-element.48) | copy-start | bytes 98308
  59.4 1.3 %copy-start.10 = (f32[64,128]{1,0:T(8,128)S(1)}, f32[64,128]{1,0:T(8,128)}, u32[]{:S(2)}) copy-start(f32[64,128]{1,0:T(8,128)} %get-tuple-element.49) | copy-start | bytes 98308
  59.6 1.2 %copy-start.5 = (f32[1,2,64,64]{3,2,1,0:T(8,128)S(1)}, f32[1,2,64,64]{3,2,1,0:T(8,128)}, u32[]{:S(2)}) copy-start(f32[1,2,64,64]{3,2,1,0:T(8,128)} %get-tuple-element.20) | copy-start | bytes 98308
  59.6 1.2 %copy-start.6 = (f32[1,2,64,64]{3,2,1,0:T(8,128)S(1)}, f32[1,2,64,64]{3,2,1,0:T(8,128)}, u32[]{:S(2)}) copy-start(f32[1,2,64,64]{3,2,1,0:T(8,128)} %get-tuple-element.21) | copy-start | bytes 98308
  60.8 1.7 %copy-start.14 = (f32[4,4]{1,0:T(4,128)S(1)}, f32[4,4]{1,0:T(4,128)}, u32[]{:S(2)}) copy-start(f32[4,4]{1,0:T(4,128)} %param.8) | copy-start | bytes 196
  63.3 1.0 copy-start
  65.5 16.1 %collective-permute-start = (f32[24,8192]{1,0:T(8,128)}, f32[24,8192]{1,0:T(8,128)S(1)}, u32[]{:S(2)}, u32[]{:S(2)}) collective-permute-start(f32[24,8192]{1,0:T(8,128)} %reshape.492), channel_id=1, source_target_pairs={{0,1},{1,2},{2,3},{3,4},{4,5},{5,6},{6,7},{7,8},{8,9},{9,10},{10,1... | collective-permute-start | bytes 2359304 | tf_op jit(solution)/shard_map/ppermute | solution.py:435
  72.8 17.5 %collective-permute-start.1 = (f32[24,8192]{1,0:T(8,128)S(1)}, f32[24,8192]{1,0:T(8,128)S(1)}, u32[]{:S(2)}, u32[]{:S(2)}) collective-permute-start(f32[24,8192]{1,0:T(8,128)S(1)} %reshape.493), channel_id=1, source_target_pairs={{1,0},{2,1},{3,2},{4,3},{5,4},{6,5},{7,6},{8,7},{9,8},{10,9},{11,1... | collective-permute-start | bytes 2359304 | tf_op jit(solution)/shard_map/ppermute | solution.py:436
  81.6 9.5 %copy-start.1 = (f32[24,8192]{1,0:T(8,128)}, f32[24,8192]{1,0:T(8,128)S(1)}, u32[]{:S(2)}) copy-start(f32[24,8192]{1,0:T(8,128)S(1)} %collective-permute-done.refs_0_.refs_1_.refs_2_) | copy-start | bytes 2359300
  90.3 0.9 copy-start.2

commit v4 on v3

--- a/solution.py
+++ b/solution.py
@@ -14,8 +14,8 @@
 SMOOTH_PASSES = 2
 
 
-HIGHEST = lax.Precision.HIGHEST
-BLOCK = 1024
+DFT_PRECISION = lax.Precision.HIGH
+BLOCK = 2048
 EDGE = 128
 CHUNK = 128
 ROWS = 8
@@ -276,13 +276,13 @@
 def spectral_core(values, phases):
     outer_size = values.shape[-2]
     inner_size = values.shape[-1]
-    values = jnp.einsum("pqkn,q...nm->p...km", dft_table(outer_size, -1), values, precision=HIGHEST)
+    values = jnp.einsum("pqkn,q...nm->p...km", dft_table(outer_size, -1), values, precision=DFT_PRECISION)
     cos_part, sin_part = twiddle(outer_size, inner_size, -1)
     values = rotate(values, cos_part, sin_part)
-    values = jnp.einsum("pqjm,q...km->p...kj", dft_table(inner_size, -1), values, precision=HIGHEST)
+    values = jnp.einsum("pqjm,q...km->p...kj", dft_table(inner_size, -1), values, precision=DFT_PRECISION)
     phase_grid = phases.reshape(inner_size, outer_size).T
     values = rotate(values, jnp.cos(phase_grid), jnp.sin(phase_grid))
-    values = jnp.einsum("pqmj,q...kj->p...km", dft_table(inner_size, 1), values, precision=HIGHEST)
+    values = jnp.einsum("pqmj,q...kj->p...km", dft_table(inner_size, 1), values, precision=DFT_PRECISION)
     cos_part, sin_part = twiddle(outer_size, inner_size, 1)
     return rotate(values, cos_part, sin_part)
 
@@ -293,7 +293,7 @@
     outer_size = length // inner_size
     spectrum = spectral_core(values.reshape(values.shape[:-1] + (outer_size, inner_size)), phases)
     result = (
-        jnp.einsum("pqnk,q...km->p...nm", dft_table(outer_size, 1), spectrum, precision=HIGHEST)
+        jnp.einsum("pqnk,q...km->p...nm", dft_table(outer_size, 1), spectrum, precision=DFT_PRECISION)
         / length
     )
     return result.reshape(values.shape)
@@ -305,7 +305,7 @@
     outer_size = length // inner_size
     spectrum = spectral_core(values.reshape(values.shape[:-1] + (outer_size, inner_size)), phases)
     inverse_rows = dft_table(outer_size, 1)
-    result = jnp.einsum("pqnk,qdlkm->pdnml", inverse_rows, spectrum, precision=HIGHEST) / length
+    result = jnp.einsum("pqnk,qdlkm->pdnml", inverse_rows, spectrum, precision=DFT_PRECISION) / length
     return result.reshape(2, values.shape[1], row_count * inner_size, values.shape[2])
 
 
@@ -315,7 +315,7 @@
     outer_size = length // inner_size
     spectrum = spectral_core(values.reshape(values.shape[:-1] + (outer_size, inner_size)), phases)
     inverse_rows = dft_table(outer_size, 1)
-    return jnp.einsum("pqnk,qdlkm->nmpdl", inverse_rows, spectrum, precision=HIGHEST) / length
+    return jnp.einsum("pqnk,qdlkm->nmpdl", inverse_rows, spectrum, precision=DFT_PRECISION) / length
 
 
 def running_window(values):

time: 114 us -> 110 us (0.965)
  matrix products: 8.83 us -> 5.7 us
where the time goes in v4:
time: 110 us; the launch traced here: 109 us
  waiting for transfers between devices  37.9 us (34%)
  starting transfers between devices  23.5 us (21%)
  Pallas kernels  20.8 us (19%)
  local copies, waits for them, and re-layouts  13.6 us (12%)
  other arithmetic  6.39 us (6%)
  matrix products  5.7 us (5%)
  between operations  1.27 us (1%)
    all_to_all x1, waiting for transfers between devices, shards(): tiles = lax.all_to_all(tiles, ('date', 'strip'), 0, 0, tiled=True)  22.3 us
    pallas_call x1, Pallas kernels, link_and_smooth(): pl.pallas_call(link_kernel, grid=(steps,), in_specs=[pl.BlockSpec((ROWS,...  20.8 us
    all_to_all x1, starting transfers between devices, shards(): tiles = lax.all_to_all(tiles, ('date', 'strip'), 0, 0, tiled=True)  14.7 us
    ppermute x1, waiting for transfers between devices, shards(): lax.ppermute(image[:, :, :halo].reshape(edge_shape), axes, [(b, a) for a,...  8.7 us
    ppermute x1, starting transfers between devices, shards(): lax.ppermute(image[:, :, column_count - halo:].reshape(edge_shape), axes,...  6.88 us
    ppermute x1, waiting for transfers between devices, shards(): lax.ppermute(image[:, :, column_count - halo:].reshape(edge_shape), axes,...  6.88 us
  transfers between devices with their start and end apart: 3, of which 3 were waited for; matrix products, arithmetic and copies ran while one was open for 5% of the time, Pallas kernels for 0%

profile of v4, /device:TPU:31, one launch (start us, length us, event | category | flops | bytes accessed | tf_op | source)
XLA Modules:
  0.0 109.1 jit_solution(16717986736470697817)
XLA Ops:
  0.6 0.1 multiply_sine_fusion.9
  0.7 0.1 fusion.55
  0.7 0.1 multiply_sine_fusion.8
  0.8 0.3 multiply_sine_fusion.1
  1.1 0.3 fusion.37
  1.3 0.3 multiply_sine_fusion
  1.6 0.3 fusion.38
  1.9 0.1 multiply_sine_fusion.7
  1.9 0.1 multiply_sine_fusion.6
  2.0 0.1 fusion.56
  2.1 1.1 %copy.47 = bf16[32,8,8,128]{3,2,1,0:T(8,128)(2,1)S(1)} copy(bf16[32,8,8,128]{3,1,2,0:T(8,128)(2,1)} %bitcast.161) | data formatting | bytes 1048576
  3.2 0.7 fusion.67
  3.9 0.1 cos.132
  4.1 0.1 sin.156
  4.2 0.5 convolution_bitcast_fusion
  4.7 0.1 multiply_subtract_fusion.5
  4.9 0.6 convolution_bitcast_fusion.7
  5.5 0.1 multiply_subtract_fusion.4
  5.7 0.6 convolution_bitcast_fusion.6
  6.3 0.1 multiply_subtract_fusion.3
  6.5 0.6 fusion.3
  7.1 1.3 %copy.14 = f32[8,128,2,2,64]{4,3,2,1,0:T(2,128)S(1)} copy(f32[8,128,2,2,64]{1,0,2,4,3:T(8,128)S(1)} %fusion.3) | data formatting | bytes 2097152 | tf_op jit(solution)/shard_map/div | solution.py:318
  8.4 2.1 %reshape.489 = f32[256,8,128]{2,1,0:T(8,128)} reshape(f32[8,128,2,2,64]{4,3,2,1,0:T(2,128)S(1)} %copy.14) | data formatting | bytes 2097152 | tf_op jit(solution)/shard_map/reshape | solution.py:417
  10.5 14.7 %all-to-all-start = ((f32[256,8,128]{2,1,0:T(8,128)}), f32[256,8,128]{2,1,0:T(8,128)S(1)}, u32[]{:S(2)}, u32[]{:S(2)}) async-start(f32[256,8,128]{2,1,0:T(8,128)} %reshape.489), calls=%async_computation | async-start | bytes 2097152 | tf_op jit(solution)/shard_map/all_to_all | solution.py:418
  25.2 0.1 fusion.66
  25.4 0.1 cos.140
  25.4 0.7 copy.18
  26.1 0.1 sin.164
  26.2 0.7 copy.19
  26.9 0.1 fusion.43
  27.1 0.1 fusion.44
  27.2 0.1 multiply_sine_fusion.5
  27.4 0.8 multiply_sine_fusion.4
  28.1 0.8 multiply_sine_fusion.3
  28.9 0.1 multiply_sine_fusion.2
  29.0 0.7 maximum_bitcast_fusion.25
  29.7 0.7 maximum_bitcast_fusion.27
  30.3 22.3 %all-to-all-done = f32[256,8,128]{2,1,0:T(8,128)S(1)} async-done(((f32[256,8,128]{2,1,0:T(8,128)}), f32[256,8,128]{2,1,0:T(8,128)S(1)}, u32[]{:S(2)}, u32[]{:S(2)}) %all-to-all-start) | async-done | bytes 1048608 | tf_op jit(solution)/shard_map/all_to_all | solution.py:418
  52.7 0.4 copy.15
  53.1 0.5 reshape.490
  53.6 0.8 copy.44
  54.4 0.3 reshape.506
  54.8 1.5 %convolution_bitcast_fusion.4 = f32[2,4,4,64,128]{4,3,0,2,1:T(8,128)S(1)} fusion(f32[2,4,4,64,128,1]{4,3,0,2,1,5:T(8,128)S(1)} %reshape.506, f32[1,2,64,64]{3,2,1,0:T(8,128)} %get-tuple-element.25, f32[1,2,64,64]{3,2,1,0:T(8,128)} %get-tuple-element.24), kind=kOutput, calls=%fused_computation.6 | convolution fusion | flops 201342976 | bytes 2162688 | tf_op jit(solution)/shard_map/pqkn,q...nm->p...km/dot_general | solution.py:279
  56.3 0.2 multiply_subtract_fusion.2
  56.5 0.6 convolution_bitcast_fusion.3
  57.2 0.2 multiply_subtract_fusion.1
  57.3 0.1 copy-done.4
  57.4 0.6 convolution_bitcast_fusion.2
  58.1 0.2 multiply_subtract_fusion
  58.3 0.0 copy-done.6
  58.3 0.6 fusion.1
  58.9 0.6 reshape.518
  59.5 0.7 copy_multiply_fusion.refs_3_.refs_4_.refs_5_
  60.2 0.5 fusion.65
  60.7 0.5 copy-done
  61.2 1.3 %reshape.492 = f32[24,8192]{1,0:T(8,128)} reshape(f32[2,4,3,8192]{3,2,1,0:T(4,128)S(1)} %get-tuple-element.15) | data formatting | bytes 1572864 | tf_op jit(solution)/shard_map/reshape | solution.py:435
  62.5 6.9 %collective-permute-start = (f32[24,8192]{1,0:T(8,128)}, f32[24,8192]{1,0:T(8,128)S(1)}, u32[]{:S(2)}, u32[]{:S(2)}) collective-permute-start(f32[24,8192]{1,0:T(8,128)} %reshape.492), channel_id=1, source_target_pairs={{0,1},{1,2},{2,3},{3,4},{4,5},{5,6},{6,7},{7,8},{8,9},{9,10},{10,1... | collective-permute-start | bytes 2359304 | tf_op jit(solution)/shard_map/ppermute | solution.py:435
  69.4 0.4 reshape.493
  69.8 1.9 %collective-permute-start.1 = (f32[24,8192]{1,0:T(8,128)S(1)}, f32[24,8192]{1,0:T(8,128)S(1)}, u32[]{:S(2)}, u32[]{:S(2)}) collective-permute-start(f32[24,8192]{1,0:T(8,128)S(1)} %reshape.493), channel_id=1, source_target_pairs={{1,0},{2,1},{3,2},{4,3},{5,4},{6,5},{7,6},{8,7},{9,8},{10,9},{11,1... | collective-permute-start | bytes 2359304 | tf_op jit(solution)/shard_map/ppermute | solution.py:436
  71.7 6.9 %collective-permute-done.refs_0_.refs_1_.refs_2_ = f32[24,8192]{1,0:T(8,128)S(1)} collective-permute-done((f32[24,8192]{1,0:T(8,128)}, f32[24,8192]{1,0:T(8,128)S(1)}, u32[]{:S(2)}, u32[]{:S(2)}) %collective-permute-start) | collective-permute-done | bytes 786464 | tf_op jit(solution)/shard_map/ppermute | solution.py:435
  78.6 8.7 %collective-permute-done.1.refs_6_.refs_7_.refs_8_ = f32[24,8192]{1,0:T(8,128)S(1)} collective-permute-done((f32[24,8192]{1,0:T(8,128)S(1)}, f32[24,8192]{1,0:T(8,128)S(1)}, u32[]{:S(2)}, u32[]{:S(2)}) %collective-permute-start.1) | collective-permute-done | bytes 786464 | tf_op jit(solution)/shard_map/ppermute | solution.py:436
  87.3 0.8 broadcast_in_dim.2.mask_ref
  88.1 0.1 copy-done.2
  88.2 20.8 %shard_map.68 = (f32[2,4,4,8192]{3,2,1,0:T(4,128)}, f32[4,8192]{1,0:T(4,128)}) custom-call(f32[8,128]{1,0:T(8,128)} %broadcast_in_dim.2.mask_ref, bf16[384,128]{1,0:T(8,128)(2,1)} %constant.136.clone.band_ref, f32[24,8192]{1,0:T(8,128)} %copy-done.1, f32[24,8192]{1,0:T(8,128)} %copy-done.1, f32[24,8192]{1,0:T(8,128)} %copy-done.1, ...), custom_call_target="tpu_custom_call" | custom-call | tf_op jit(solution)/shard_map/pallas_call | solution.py:182
  (33 shorter events, 0.2 us)
Async XLA Ops:
  5.7 0.8 copy-start.3
  8.4 16.8 %copy-start.13 = (f32[8192]{0:T(1024)S(1)}, f32[8192]{0:T(1024)}, u32[]{:S(2)}) copy-start(f32[8192]{0:T(1024)} %param.7) | copy-start | bytes 98308
  10.5 42.1 %all-to-all-start = ((f32[256,8,128]{2,1,0:T(8,128)}), f32[256,8,128]{2,1,0:T(8,128)S(1)}, u32[]{:S(2)}, u32[]{:S(2)}) async-start(f32[256,8,128]{2,1,0:T(8,128)} %reshape.489), calls=%async_computation | async-start | bytes 2097152 | tf_op jit(solution)/shard_map/all_to_all | solution.py:418
  54.8 1.5 %copy-start.11 = (f32[64,128]{1,0:T(8,128)S(1)}, f32[64,128]{1,0:T(8,128)}, u32[]{:S(2)}) copy-start(f32[64,128]{1,0:T(8,128)} %get-tuple-element.46) | copy-start | bytes 98308
  54.8 1.5 %copy-start.12 = (f32[64,128]{1,0:T(8,128)S(1)}, f32[64,128]{1,0:T(8,128)}, u32[]{:S(2)}) copy-start(f32[64,128]{1,0:T(8,128)} %get-tuple-element.47) | copy-start | bytes 98308
  56.3 0.8 copy-start.7
  56.3 0.8 copy-start.8
  56.5 0.9 copy-start.4
  57.1 0.9 copy-start.9
  57.2 0.9 copy-start.10
  57.4 0.8 copy-start.5
  57.4 0.9 copy-start.6
  58.3 1.2 %copy-start.14 = (f32[4,4]{1,0:T(4,128)S(1)}, f32[4,4]{1,0:T(4,128)}, u32[]{:S(2)}) copy-start(f32[4,4]{1,0:T(4,128)} %param.8) | copy-start | bytes 196
  60.2 1.0 copy-start
  62.5 16.1 %collective-permute-start = (f32[24,8192]{1,0:T(8,128)}, f32[24,8192]{1,0:T(8,128)S(1)}, u32[]{:S(2)}, u32[]{:S(2)}) collective-permute-start(f32[24,8192]{1,0:T(8,128)} %reshape.492), channel_id=1, source_target_pairs={{0,1},{1,2},{2,3},{3,4},{4,5},{5,6},{6,7},{7,8},{8,9},{9,10},{10,1... | collective-permute-start | bytes 2359304 | tf_op jit(solution)/shard_map/ppermute | solution.py:435
  69.8 17.5 %collective-permute-start.1 = (f32[24,8192]{1,0:T(8,128)S(1)}, f32[24,8192]{1,0:T(8,128)S(1)}, u32[]{:S(2)}, u32[]{:S(2)}) collective-permute-start(f32[24,8192]{1,0:T(8,128)S(1)} %reshape.493), channel_id=1, source_target_pairs={{1,0},{2,1},{3,2},{4,3},{5,4},{6,5},{7,6},{8,7},{9,8},{10,9},{11,1... | collective-permute-start | bytes 2359304 | tf_op jit(solution)/shard_map/ppermute | solution.py:436
  78.6 9.5 %copy-start.1 = (f32[24,8192]{1,0:T(8,128)}, f32[24,8192]{1,0:T(8,128)S(1)}, u32[]{:S(2)}) copy-start(f32[24,8192]{1,0:T(8,128)S(1)} %collective-permute-done.refs_0_.refs_1_.refs_2_) | copy-start | bytes 2359300
  87.3 0.9 copy-start.2

commit v5 on v4

--- a/solution.py
+++ b/solution.py
@@ -23,7 +23,7 @@
 
 def link_kernel(mask_ref, band_ref, *refs):
     pieces = refs[:9]
-    vec_ref, qual_ref, image, terms, high, low, sums = refs[9:]
+    vec_ref, qual_ref, image, high, low, sums = refs[9:]
     step = pl.program_id(0)
     last = pl.num_programs(0) - 1
     dates = pieces[4].shape[1]
@@ -55,29 +55,45 @@
         specs.append((1, a, b))
         specs.append((2, a, b))
 
-    for number, (kind, a, b) in enumerate(specs):
-        ra, ia = image[0, a], image[1, a]
+    def product(kind, a, b, rows, lanes):
+        ra, ia = image[0, a, rows, lanes], image[1, a, rows, lanes]
         if kind == 0:
-            value = ra * ra + ia * ia
-        else:
-            rb, ib = image[0, b], image[1, b]
-            if kind == 1:
-                value = ra * rb + ia * ib
-            else:
-                value = ia * rb - ra * ib
-        across = value + pltpu.roll(value, padded - 1, 0) + pltpu.roll(value, padded - 2, 0)
-        terms[number * ROWS : (number + 1) * ROWS, :] = across[:ROWS]
-    full = terms[...]
-    top = full.astype(jnp.bfloat16)
-    high[...] = top
-    low[...] = (full - top.astype(jnp.float32)).astype(jnp.bfloat16)
+            return ra * ra + ia * ia
+        rb, ib = image[0, b, rows, lanes], image[1, b, rows, lanes]
+        if kind == 1:
+            return ra * rb + ia * ib
+        return ia * rb - ra * ib
+
+    row_index = lax.broadcasted_iota(jnp.int32, (ROWS, CHUNK), 0)
+
+    def term_body(column):
+        lanes = slice(column * CHUNK, (column + 1) * CHUNK)
+        sums_of_pair = []
+        for number, (kind, a, b) in enumerate(specs):
+            upper = product(kind, a, b, slice(0, ROWS), lanes)
+            lower = product(kind, a, b, slice(ROWS, 2 * ROWS), lanes)
+            one = jnp.where(row_index < ROWS - 1, pltpu.roll(upper, ROWS - 1, 0), pltpu.roll(lower, ROWS - 1, 0))
+            two = jnp.where(row_index < ROWS - 2, pltpu.roll(upper, ROWS - 2, 0), pltpu.roll(lower, ROWS - 2, 0))
+            sums_of_pair.append(upper + one + two)
+            if len(sums_of_pair) == 2:
+                full = jnp.concatenate(sums_of_pair, axis=0)
+                top = full.astype(jnp.bfloat16)
+                rows = slice((number - 1) * ROWS, (number + 1) * ROWS)
+                high[rows, lanes] = top
+                low[rows, lanes] = (full - top.astype(jnp.float32)).astype(jnp.bfloat16)
+                sums_of_pair = []
+
+        if column >= 2:
+            left = (column - 2) * CHUNK
+            window = jnp.dot(high[:, left : left + CHUNK + 2 * EDGE], band, preferred_element_type=jnp.float32)
+            window = window + jnp.dot(
+                low[:, left : left + CHUNK + 2 * EDGE], band, preferred_element_type=jnp.float32
+            )
+            sums[:, left : left + CHUNK] = window
+
     band = band_ref[...]
-    for index in range(block // CHUNK):
-        left = index * CHUNK
-        window = jnp.dot(high[:, left : left + CHUNK + 2 * EDGE], band, preferred_element_type=jnp.float32)
-        window = window + jnp.dot(low[:, left : left + CHUNK + 2 * EDGE], band, preferred_element_type=jnp.float32)
-        sums[:, left : left + CHUNK] = window
-
+    for column in range(image.shape[3] // CHUNK):
+        term_body(column)
     mask = mask_ref[...]
     inverse_scale = 1.0 / (3 * (2 * WIN_HALF + 1))
 
@@ -153,7 +169,7 @@
         qual_ref[:, pl.ds(start, CHUNK)] = quality[keep]
         return carry
 
-    lax.fori_loop(0, block // CHUNK, chunk_body, 0)
+    lax.fori_loop(0, block // CHUNK, chunk_body, 0, unroll=4)
 
 
 def link_and_smooth(pieces, valid_mask):
@@ -197,7 +213,6 @@
         ],
         scratch_shapes=[
             pltpu.VMEM((parts, dates, padded, width), jnp.float32),
-            pltpu.VMEM((term_count * ROWS, width), jnp.float32),
             pltpu.VMEM((term_count * ROWS, width), jnp.bfloat16),
             pltpu.VMEM((term_count * ROWS, width), jnp.bfloat16),
             pltpu.VMEM((term_count * ROWS, BLOCK), jnp.float32),

time: 110 us -> 105 us (0.955)
  Pallas kernels: 20.8 us -> 16.6 us
    pallas_call x1, Pallas kernels: 20.8 us -> 16.6 us  [link_and_smooth(): pl.pallas_call(link_kernel, grid=(steps,), in_specs=[pl.BlockSpec((ROWS,...]
where the time goes in v5:
time: 105 us
  waiting for transfers between devices  37.9 us (36%)
  starting transfers between devices  23.5 us (22%)
  Pallas kernels  16.6 us (16%)
  local copies, waits for them, and re-layouts  13.6 us (13%)
  other arithmetic  6.39 us (6%)
  matrix products  5.7 us (5%)
  between operations  1.27 us (1%)
    all_to_all x1, waiting for transfers between devices, shards(): tiles = lax.all_to_all(tiles, ('date', 'strip'), 0, 0, tiled=True)  22.3 us
    pallas_call x1, Pallas kernels, link_and_smooth(): pl.pallas_call(link_kernel, grid=(steps,), in_specs=[pl.BlockSpec((ROWS,...  16.6 us
    all_to_all x1, starting transfers between devices, shards(): tiles = lax.all_to_all(tiles, ('date', 'strip'), 0, 0, tiled=True)  14.7 us
    ppermute x1, waiting for transfers between devices, shards(): lax.ppermute(image[:, :, :halo].reshape(edge_shape), axes, [(b, a) for a,...  8.7 us
    ppermute x1, starting transfers between devices, shards(): lax.ppermute(image[:, :, column_count - halo:].reshape(edge_shape), axes,...  6.88 us
    ppermute x1, waiting for transfers between devices, shards(): lax.ppermute(image[:, :, column_count - halo:].reshape(edge_shape), axes,...  6.88 us
    reshape x1, local copies, waits for them, and re-layouts, shards(): tiles = ranged.reshape(devices, -1, 128)  2.13 us
  transfers between devices with their start and end apart: 3, of which 3 were waited for; matrix products, arithmetic and copies ran while one was open for 5% of the time, Pallas kernels for 0%

profile of v5, /device:TPU:31, one launch (start us, length us, event | category | flops | bytes accessed | tf_op | source)
XLA Modules:
  0.0 105.0 jit_solution(14151682230515059104)
XLA Ops:
  0.6 0.1 multiply_sine_fusion.9
  0.7 0.1 fusion.55
  0.7 0.1 multiply_sine_fusion.8
  0.8 0.3 multiply_sine_fusion.1
  1.1 0.3 fusion.37
  1.3 0.3 multiply_sine_fusion
  1.6 0.3 fusion.38
  1.9 0.1 multiply_sine_fusion.7
  1.9 0.1 multiply_sine_fusion.6
  2.0 0.1 fusion.56
  2.1 1.1 %copy.47 = bf16[32,8,8,128]{3,2,1,0:T(8,128)(2,1)S(1)} copy(bf16[32,8,8,128]{3,1,2,0:T(8,128)(2,1)} %bitcast.161) | data formatting | bytes 1048576
  3.2 0.7 fusion.67
  3.9 0.1 cos.132
  4.1 0.1 sin.156
  4.2 0.5 convolution_bitcast_fusion
  4.7 0.1 multiply_subtract_fusion.5
  4.9 0.6 convolution_bitcast_fusion.7
  5.5 0.1 multiply_subtract_fusion.4
  5.7 0.6 convolution_bitcast_fusion.6
  6.3 0.1 multiply_subtract_fusion.3
  6.5 0.6 fusion.3
  7.1 1.3 %copy.14 = f32[8,128,2,2,64]{4,3,2,1,0:T(2,128)S(1)} copy(f32[8,128,2,2,64]{1,0,2,4,3:T(8,128)S(1)} %fusion.3) | data formatting | bytes 2097152 | tf_op jit(solution)/shard_map/div | solution.py:333
  8.4 2.1 %reshape.489 = f32[256,8,128]{2,1,0:T(8,128)} reshape(f32[8,128,2,2,64]{4,3,2,1,0:T(2,128)S(1)} %copy.14) | data formatting | bytes 2097152 | tf_op jit(solution)/shard_map/reshape | solution.py:432
  10.5 14.7 %all-to-all-start = ((f32[256,8,128]{2,1,0:T(8,128)}), f32[256,8,128]{2,1,0:T(8,128)S(1)}, u32[]{:S(2)}, u32[]{:S(2)}) async-start(f32[256,8,128]{2,1,0:T(8,128)} %reshape.489), calls=%async_computation | async-start | bytes 2097152 | tf_op jit(solution)/shard_map/all_to_all | solution.py:433
  25.2 0.1 fusion.66
  25.4 0.1 cos.140
  25.4 0.7 copy.18
  26.1 0.1 sin.164
  26.2 0.7 copy.19
  26.9 0.1 fusion.43
  27.1 0.1 fusion.44
  27.2 0.1 multiply_sine_fusion.5
  27.4 0.8 multiply_sine_fusion.4
  28.1 0.8 multiply_sine_fusion.3
  28.9 0.1 multiply_sine_fusion.2
  29.0 0.7 maximum_bitcast_fusion.25
  29.7 0.7 maximum_bitcast_fusion.27
  30.3 22.3 %all-to-all-done = f32[256,8,128]{2,1,0:T(8,128)S(1)} async-done(((f32[256,8,128]{2,1,0:T(8,128)}), f32[256,8,128]{2,1,0:T(8,128)S(1)}, u32[]{:S(2)}, u32[]{:S(2)}) %all-to-all-start) | async-done | bytes 1048608 | tf_op jit(solution)/shard_map/all_to_all | solution.py:433
  52.7 0.4 copy.15
  53.1 0.5 reshape.490
  53.6 0.8 copy.44
  54.4 0.3 reshape.506
  54.8 1.5 %convolution_bitcast_fusion.4 = f32[2,4,4,64,128]{4,3,0,2,1:T(8,128)S(1)} fusion(f32[2,4,4,64,128,1]{4,3,0,2,1,5:T(8,128)S(1)} %reshape.506, f32[1,2,64,64]{3,2,1,0:T(8,128)} %get-tuple-element.25, f32[1,2,64,64]{3,2,1,0:T(8,128)} %get-tuple-element.24), kind=kOutput, calls=%fused_computation.6 | convolution fusion | flops 201342976 | bytes 2162688 | tf_op jit(solution)/shard_map/pqkn,q...nm->p...km/dot_general | solution.py:294
  56.3 0.2 multiply_subtract_fusion.2
  56.5 0.6 convolution_bitcast_fusion.3
  57.2 0.2 multiply_subtract_fusion.1
  57.3 0.1 copy-done.4
  57.4 0.6 convolution_bitcast_fusion.2
  58.1 0.2 multiply_subtract_fusion
  58.3 0.0 copy-done.6
  58.3 0.6 fusion.1
  58.9 0.6 reshape.518
  59.5 0.7 copy_multiply_fusion.refs_3_.refs_4_.refs_5_
  60.2 0.5 fusion.65
  60.7 0.5 copy-done
  61.2 1.3 %reshape.492 = f32[24,8192]{1,0:T(8,128)} reshape(f32[2,4,3,8192]{3,2,1,0:T(4,128)S(1)} %get-tuple-element.15) | data formatting | bytes 1572864 | tf_op jit(solution)/shard_map/reshape | solution.py:450
  62.5 6.9 %collective-permute-start = (f32[24,8192]{1,0:T(8,128)}, f32[24,8192]{1,0:T(8,128)S(1)}, u32[]{:S(2)}, u32[]{:S(2)}) collective-permute-start(f32[24,8192]{1,0:T(8,128)} %reshape.492), channel_id=1, source_target_pairs={{0,1},{1,2},{2,3},{3,4},{4,5},{5,6},{6,7},{7,8},{8,9},{9,10},{10,1... | collective-permute-start | bytes 2359304 | tf_op jit(solution)/shard_map/ppermute | solution.py:450
  69.4 0.4 reshape.493
  69.8 1.9 %collective-permute-start.1 = (f32[24,8192]{1,0:T(8,128)S(1)}, f32[24,8192]{1,0:T(8,128)S(1)}, u32[]{:S(2)}, u32[]{:S(2)}) collective-permute-start(f32[24,8192]{1,0:T(8,128)S(1)} %reshape.493), channel_id=1, source_target_pairs={{1,0},{2,1},{3,2},{4,3},{5,4},{6,5},{7,6},{8,7},{9,8},{10,9},{11,1... | collective-permute-start | bytes 2359304 | tf_op jit(solution)/shard_map/ppermute | solution.py:451
  71.7 6.9 %collective-permute-done.refs_0_.refs_1_.refs_2_ = f32[24,8192]{1,0:T(8,128)S(1)} collective-permute-done((f32[24,8192]{1,0:T(8,128)}, f32[24,8192]{1,0:T(8,128)S(1)}, u32[]{:S(2)}, u32[]{:S(2)}) %collective-permute-start) | collective-permute-done | bytes 786464 | tf_op jit(solution)/shard_map/ppermute | solution.py:450
  78.6 8.7 %collective-permute-done.1.refs_6_.refs_7_.refs_8_ = f32[24,8192]{1,0:T(8,128)S(1)} collective-permute-done((f32[24,8192]{1,0:T(8,128)S(1)}, f32[24,8192]{1,0:T(8,128)S(1)}, u32[]{:S(2)}, u32[]{:S(2)}) %collective-permute-start.1) | collective-permute-done | bytes 786464 | tf_op jit(solution)/shard_map/ppermute | solution.py:451
  87.3 0.8 broadcast_in_dim.2.mask_ref
  88.1 0.1 copy-done.2
  88.2 16.6 %shard_map.68 = (f32[2,4,4,8192]{3,2,1,0:T(4,128)}, f32[4,8192]{1,0:T(4,128)}) custom-call(f32[8,128]{1,0:T(8,128)} %broadcast_in_dim.2.mask_ref, bf16[384,128]{1,0:T(8,128)(2,1)} %constant.136.clone.band_ref, f32[24,8192]{1,0:T(8,128)} %copy-done.1, f32[24,8192]{1,0:T(8,128)} %copy-done.1, f32[24,8192]{1,0:T(8,128)} %copy-done.1, ...), custom_call_target="tpu_custom_call" | custom-call | tf_op jit(solution)/shard_map/pallas_call | solution.py:198
  (33 shorter events, 0.2 us)
Async XLA Ops:
  5.7 0.8 copy-start.3
  8.4 16.8 %copy-start.13 = (f32[8192]{0:T(1024)S(1)}, f32[8192]{0:T(1024)}, u32[]{:S(2)}) copy-start(f32[8192]{0:T(1024)} %param.7) | copy-start | bytes 98308
  10.5 42.1 %all-to-all-start = ((f32[256,8,128]{2,1,0:T(8,128)}), f32[256,8,128]{2,1,0:T(8,128)S(1)}, u32[]{:S(2)}, u32[]{:S(2)}) async-start(f32[256,8,128]{2,1,0:T(8,128)} %reshape.489), calls=%async_computation | async-start | bytes 2097152 | tf_op jit(solution)/shard_map/all_to_all | solution.py:433
  54.8 1.5 %copy-start.11 = (f32[64,128]{1,0:T(8,128)S(1)}, f32[64,128]{1,0:T(8,128)}, u32[]{:S(2)}) copy-start(f32[64,128]{1,0:T(8,128)} %get-tuple-element.46) | copy-start | bytes 98308
  54.8 1.5 %copy-start.12 = (f32[64,128]{1,0:T(8,128)S(1)}, f32[64,128]{1,0:T(8,128)}, u32[]{:S(2)}) copy-start(f32[64,128]{1,0:T(8,128)} %get-tuple-element.47) | copy-start | bytes 98308
  56.3 0.8 copy-start.7
  56.3 0.8 copy-start.8
  56.5 0.9 copy-start.4
  57.1 0.9 copy-start.9
  57.2 0.9 copy-start.10
  57.4 0.8 copy-start.5
  57.4 0.9 copy-start.6
  58.3 1.2 %copy-start.14 = (f32[4,4]{1,0:T(4,128)S(1)}, f32[4,4]{1,0:T(4,128)}, u32[]{:S(2)}) copy-start(f32[4,4]{1,0:T(4,128)} %param.8) | copy-start | bytes 196
  60.2 1.0 copy-start
  62.5 16.1 %collective-permute-start = (f32[24,8192]{1,0:T(8,128)}, f32[24,8192]{1,0:T(8,128)S(1)}, u32[]{:S(2)}, u32[]{:S(2)}) collective-permute-start(f32[24,8192]{1,0:T(8,128)} %reshape.492), channel_id=1, source_target_pairs={{0,1},{1,2},{2,3},{3,4},{4,5},{5,6},{6,7},{7,8},{8,9},{9,10},{10,1... | collective-permute-start | bytes 2359304 | tf_op jit(solution)/shard_map/ppermute | solution.py:450
  69.8 17.5 %collective-permute-start.1 = (f32[24,8192]{1,0:T(8,128)S(1)}, f32[24,8192]{1,0:T(8,128)S(1)}, u32[]{:S(2)}, u32[]{:S(2)}) collective-permute-start(f32[24,8192]{1,0:T(8,128)S(1)} %reshape.493), channel_id=1, source_target_pairs={{1,0},{2,1},{3,2},{4,3},{5,4},{6,5},{7,6},{8,7},{9,8},{10,9},{11,1... | collective-permute-start | bytes 2359304 | tf_op jit(solution)/shard_map/ppermute | solution.py:451
  78.6 9.5 %copy-start.1 = (f32[24,8192]{1,0:T(8,128)}, f32[24,8192]{1,0:T(8,128)S(1)}, u32[]{:S(2)}) copy-start(f32[24,8192]{1,0:T(8,128)S(1)} %collective-permute-done.refs_0_.refs_1_.refs_2_) | copy-start | bytes 2359300
  87.3 0.9 copy-start.2

commit v6 on v5

--- a/solution.py
+++ b/solution.py
@@ -1,3 +1,4 @@
+import functools
 import math
 
 import numpy as np
@@ -21,7 +22,7 @@
 ROWS = 8
 
 
-def link_kernel(mask_ref, band_ref, *refs):
+def link_kernel(column_count, total_columns, band_ref, *refs):
     pieces = refs[:9]
     vec_ref, qual_ref, image, high, low, sums = refs[9:]
     step = pl.program_id(0)
@@ -94,7 +95,9 @@
     band = band_ref[...]
     for column in range(image.shape[3] // CHUNK):
         term_body(column)
-    mask = mask_ref[...]
+    device = lax.axis_index("date") * lax.axis_size("strip") + lax.axis_index("strip")
+    columns = device * column_count - SMOOTH_PASSES + lax.broadcasted_iota(jnp.int32, (ROWS, CHUNK), 0)
+    mask = ((columns >= 0) & (columns < total_columns)).astype(jnp.float32)
     inverse_scale = 1.0 / (3 * (2 * WIN_HALF + 1))
 
     def chunk_body(index, carry):
@@ -172,7 +175,7 @@
     lax.fori_loop(0, block // CHUNK, chunk_body, 0, unroll=4)
 
 
-def link_and_smooth(pieces, valid_mask):
+def link_and_smooth(pieces, column_count, total_columns):
     parts, dates, _, lines = pieces[1].shape
     assert all(piece.shape[-1] == lines for piece in pieces)
     padded = 16
@@ -181,7 +184,6 @@
     per_block = BLOCK // EDGE
     edges = lines // EDGE
     term_count = dates + dates * (dates - 1)
-    mask = jnp.broadcast_to(valid_mask[:, None], (ROWS, CHUNK))
     offset = np.arange(CHUNK + 2 * EDGE)[:, None] - EDGE - np.arange(CHUNK)[None, :]
     band = jnp.asarray(np.abs(offset) <= WIN_HALF, jnp.bfloat16)
     width = BLOCK + 2 * EDGE
@@ -196,10 +198,9 @@
         ]
         operands += [piece, piece, piece]
     return pl.pallas_call(
-        link_kernel,
+        functools.partial(link_kernel, column_count, total_columns),
         grid=(steps,),
         in_specs=[
-            pl.BlockSpec((ROWS, CHUNK), lambda i: (0, 0)),
             pl.BlockSpec((CHUNK + 2 * EDGE, CHUNK), lambda i: (0, 0)),
         ]
         + piece_specs,
@@ -217,7 +218,7 @@
             pltpu.VMEM((term_count * ROWS, width), jnp.bfloat16),
             pltpu.VMEM((term_count * ROWS, BLOCK), jnp.float32),
         ],
-    )(mask, band, *operands)
+    )(band, *operands)
 
 
 def split_up(x, dim, count):
@@ -450,10 +451,7 @@
     low = lax.ppermute(image[:, :, column_count - halo :].reshape(edge_shape), axes, up)
     high = lax.ppermute(image[:, :, :halo].reshape(edge_shape), axes, [(b, a) for a, b in up])
     total_columns = column_count * lax.axis_size("date") * lax.axis_size("strip")
-    first = lax.axis_index(("date", "strip")) * column_count - SMOOTH_PASSES
-    columns = first + jnp.arange(column_count + 2 * SMOOTH_PASSES, dtype=jnp.int32)
-    valid_mask = ((columns >= 0) & (columns < total_columns)).astype(jnp.float32)
-    vector, quality = link_and_smooth((low, image, high), valid_mask)
+    vector, quality = link_and_smooth((low, image, high), column_count, total_columns)
     return (vector, quality)
 
 

time: 105 us -> 105 us (level)
  no operation moved by 1% of the time
where the time goes in v6:
time: 105 us
  waiting for transfers between devices  37.9 us (36%)
  starting transfers between devices  23.5 us (22%)
  Pallas kernels  16.7 us (16%)
  local copies, waits for them, and re-layouts  13.6 us (13%)
  other arithmetic  6.38 us (6%)
  matrix products  5.7 us (5%)
  between operations  1.25 us (1%)
    all_to_all x1, waiting for transfers between devices, shards(): tiles = lax.all_to_all(tiles, ('date', 'strip'), 0, 0, tiled=True)  22.3 us
    pallas_call x1, Pallas kernels, link_and_smooth(): pl.pallas_call(functools.partial(link_kernel, column_count, total_columns...  16.7 us
    all_to_all x1, starting transfers between devices, shards(): tiles = lax.all_to_all(tiles, ('date', 'strip'), 0, 0, tiled=True)  14.7 us
    ppermute x1, waiting for transfers between devices, shards(): lax.ppermute(image[:, :, :halo].reshape(edge_shape), axes, [(b, a) for a,...  8.7 us
    ppermute x1, waiting for transfers between devices, shards(): lax.ppermute(image[:, :, column_count - halo:].reshape(edge_shape), axes,...  6.9 us
    ppermute x1, starting transfers between devices, shards(): lax.ppermute(image[:, :, column_count - halo:].reshape(edge_shape), axes,...  6.88 us
    unnamed x31, local copies, waits for them, and re-layouts  2.68 us
    reshape x1, local copies, waits for them, and re-layouts, shards(): tiles = ranged.reshape(devices, -1, 128)  2.13 us
  transfers between devices with their start and end apart: 3, of which 3 were waited for; matrix products, arithmetic and copies ran while one was open for 5% of the time, Pallas kernels for 0%

profile of v6, /device:TPU:31, one launch (start us, length us, event | category | flops | bytes accessed | tf_op | source)
XLA Modules:
  0.0 105.0 jit_solution(11963004566649549693)
XLA Ops:
  0.6 0.1 multiply_sine_fusion.9
  0.7 0.1 fusion.55
  0.7 0.1 multiply_sine_fusion.8
  0.8 0.3 multiply_sine_fusion.1
  1.1 0.3 fusion.37
  1.3 0.3 multiply_sine_fusion
  1.6 0.3 fusion.38
  1.9 0.1 multiply_sine_fusion.7
  1.9 0.1 multiply_sine_fusion.6
  2.0 0.1 fusion.56
  2.1 1.1 %copy.47 = bf16[32,8,8,128]{3,2,1,0:T(8,128)(2,1)S(1)} copy(bf16[32,8,8,128]{3,1,2,0:T(8,128)(2,1)} %bitcast.161) | data formatting | bytes 1048576
  3.2 0.7 fusion.67
  3.9 0.1 cos.132
  4.1 0.1 sin.156
  4.2 0.5 convolution_bitcast_fusion
  4.7 0.1 multiply_subtract_fusion.5
  4.9 0.6 convolution_bitcast_fusion.7
  5.5 0.1 multiply_subtract_fusion.4
  5.7 0.6 convolution_bitcast_fusion.6
  6.3 0.1 multiply_subtract_fusion.3
  6.4 0.6 fusion.3
  7.1 1.3 %copy.14 = f32[8,128,2,2,64]{4,3,2,1,0:T(2,128)S(1)} copy(f32[8,128,2,2,64]{1,0,2,4,3:T(8,128)S(1)} %fusion.3) | data formatting | bytes 2097152 | tf_op jit(solution)/shard_map/div | solution.py:334
  8.4 2.1 %reshape.481 = f32[256,8,128]{2,1,0:T(8,128)} reshape(f32[8,128,2,2,64]{4,3,2,1,0:T(2,128)S(1)} %copy.14) | data formatting | bytes 2097152 | tf_op jit(solution)/shard_map/reshape | solution.py:433
  10.5 14.7 %all-to-all-start = ((f32[256,8,128]{2,1,0:T(8,128)}), f32[256,8,128]{2,1,0:T(8,128)S(1)}, u32[]{:S(2)}, u32[]{:S(2)}) async-start(f32[256,8,128]{2,1,0:T(8,128)} %reshape.481), calls=%async_computation | async-start | bytes 2097152 | tf_op jit(solution)/shard_map/all_to_all | solution.py:434
  25.2 0.1 fusion.66
  25.4 0.1 cos.140
  25.4 0.7 copy.18
  26.1 0.1 sin.164
  26.2 0.7 copy.19
  26.9 0.1 fusion.43
  27.1 0.1 fusion.44
  27.2 0.1 multiply_sine_fusion.5
  27.4 0.8 multiply_sine_fusion.4
  28.1 0.8 multiply_sine_fusion.3
  28.9 0.1 multiply_sine_fusion.2
  29.0 0.7 maximum_bitcast_fusion.25
  29.7 0.7 maximum_bitcast_fusion.27
  30.3 22.3 %all-to-all-done = f32[256,8,128]{2,1,0:T(8,128)S(1)} async-done(((f32[256,8,128]{2,1,0:T(8,128)}), f32[256,8,128]{2,1,0:T(8,128)S(1)}, u32[]{:S(2)}, u32[]{:S(2)}) %all-to-all-start) | async-done | bytes 1048608 | tf_op jit(solution)/shard_map/all_to_all | solution.py:434
  52.7 0.4 copy.15
  53.1 0.5 reshape.482
  53.6 0.8 copy.44
  54.4 0.3 reshape.498
  54.8 1.5 %convolution_bitcast_fusion.4 = f32[2,4,4,64,128]{4,3,0,2,1:T(8,128)S(1)} fusion(f32[2,4,4,64,128,1]{4,3,0,2,1,5:T(8,128)S(1)} %reshape.498, f32[1,2,64,64]{3,2,1,0:T(8,128)} %get-tuple-element.25, f32[1,2,64,64]{3,2,1,0:T(8,128)} %get-tuple-element.24), kind=kOutput, calls=%fused_computation.6 | convolution fusion | flops 201342976 | bytes 2162688 | tf_op jit(solution)/shard_map/pqkn,q...nm->p...km/dot_general | solution.py:295
  56.3 0.2 multiply_subtract_fusion.2
  56.5 0.6 convolution_bitcast_fusion.3
  57.2 0.2 multiply_subtract_fusion.1
  57.3 0.1 copy-done.4
  57.4 0.6 convolution_bitcast_fusion.2
  58.1 0.2 multiply_subtract_fusion
  58.2 0.0 copy-done.5
  58.3 0.0 copy-done.6
  58.3 0.6 fusion.1
  58.9 0.6 reshape.510
  59.5 0.7 copy_multiply_fusion.refs_3_.refs_4_.refs_5_
  60.2 0.5 fusion.65
  60.7 0.5 copy-done
  61.2 1.3 %reshape.484 = f32[24,8192]{1,0:T(8,128)} reshape(f32[2,4,3,8192]{3,2,1,0:T(4,128)S(1)} %get-tuple-element.15) | data formatting | bytes 1572864 | tf_op jit(solution)/shard_map/reshape | solution.py:451
  62.5 6.9 %collective-permute-start = (f32[24,8192]{1,0:T(8,128)}, f32[24,8192]{1,0:T(8,128)S(1)}, u32[]{:S(2)}, u32[]{:S(2)}) collective-permute-start(f32[24,8192]{1,0:T(8,128)} %reshape.484), channel_id=1, source_target_pairs={{0,1},{1,2},{2,3},{3,4},{4,5},{5,6},{6,7},{7,8},{8,9},{9,10},{10,1... | collective-permute-start | bytes 2359304 | tf_op jit(solution)/shard_map/ppermute | solution.py:451
  69.4 0.4 reshape.485
  69.8 1.9 %collective-permute-start.1 = (f32[24,8192]{1,0:T(8,128)S(1)}, f32[24,8192]{1,0:T(8,128)S(1)}, u32[]{:S(2)}, u32[]{:S(2)}) collective-permute-start(f32[24,8192]{1,0:T(8,128)S(1)} %reshape.485), channel_id=1, source_target_pairs={{1,0},{2,1},{3,2},{4,3},{5,4},{6,5},{7,6},{8,7},{9,8},{10,9},{11,1... | collective-permute-start | bytes 2359304 | tf_op jit(solution)/shard_map/ppermute | solution.py:452
  71.7 6.9 %collective-permute-done.refs_0_.refs_1_.refs_2_ = f32[24,8192]{1,0:T(8,128)S(1)} collective-permute-done((f32[24,8192]{1,0:T(8,128)}, f32[24,8192]{1,0:T(8,128)S(1)}, u32[]{:S(2)}, u32[]{:S(2)}) %collective-permute-start) | collective-permute-done | bytes 786464 | tf_op jit(solution)/shard_map/ppermute | solution.py:451
  78.6 8.7 %collective-permute-done.1.refs_6_.refs_7_.refs_8_ = f32[24,8192]{1,0:T(8,128)S(1)} collective-permute-done((f32[24,8192]{1,0:T(8,128)S(1)}, f32[24,8192]{1,0:T(8,128)S(1)}, u32[]{:S(2)}, u32[]{:S(2)}) %collective-permute-start.1) | collective-permute-done | bytes 786464 | tf_op jit(solution)/shard_map/ppermute | solution.py:452
  87.3 0.9 copy-done.2
  88.2 16.7 %shard_map.68 = (f32[2,4,4,8192]{3,2,1,0:T(4,128)}, f32[4,8192]{1,0:T(4,128)}) custom-call(bf16[384,128]{1,0:T(8,128)(2,1)} %constant.120.clone.band_ref, f32[24,8192]{1,0:T(8,128)} %copy-done.1, f32[24,8192]{1,0:T(8,128)} %copy-done.1, f32[24,8192]{1,0:T(8,128)} %copy-done.1, f32[2,4,4,8192]{3,2,1,0:T(4,128)} %copy-done, f32[2,4,4,8192]{3,2,1,0:T(4,128)} %copy-done, ...), custom_call_target="tpu_custom_call" | custom-call | tf_op jit(solution)/shard_map/pallas_call | solution.py:200
  (31 shorter events, 0.2 us)
Async XLA Ops:
  5.7 0.8 copy-start.3
  8.4 16.8 %copy-start.13 = (f32[8192]{0:T(1024)S(1)}, f32[8192]{0:T(1024)}, u32[]{:S(2)}) copy-start(f32[8192]{0:T(1024)} %param.7) | copy-start | bytes 98308
  10.5 42.1 %all-to-all-start = ((f32[256,8,128]{2,1,0:T(8,128)}), f32[256,8,128]{2,1,0:T(8,128)S(1)}, u32[]{:S(2)}, u32[]{:S(2)}) async-start(f32[256,8,128]{2,1,0:T(8,128)} %reshape.481), calls=%async_computation | async-start | bytes 2097152 | tf_op jit(solution)/shard_map/all_to_all | solution.py:434
  54.8 1.5 %copy-start.11 = (f32[64,128]{1,0:T(8,128)S(1)}, f32[64,128]{1,0:T(8,128)}, u32[]{:S(2)}) copy-start(f32[64,128]{1,0:T(8,128)} %get-tuple-element.46) | copy-start | bytes 98308
  54.8 1.5 %copy-start.12 = (f32[64,128]{1,0:T(8,128)S(1)}, f32[64,128]{1,0:T(8,128)}, u32[]{:S(2)}) copy-start(f32[64,128]{1,0:T(8,128)} %get-tuple-element.47) | copy-start | bytes 98308
  56.3 0.8 copy-start.7
  56.3 0.8 copy-start.8
  56.5 0.9 copy-start.4
  57.1 0.9 copy-start.9
  57.2 0.9 copy-start.10
  57.4 0.8 copy-start.5
  57.4 0.9 copy-start.6
  58.3 1.2 %copy-start.14 = (f32[4,4]{1,0:T(4,128)S(1)}, f32[4,4]{1,0:T(4,128)}, u32[]{:S(2)}) copy-start(f32[4,4]{1,0:T(4,128)} %param.8) | copy-start | bytes 196
  60.2 1.0 copy-start
  62.5 16.1 %collective-permute-start = (f32[24,8192]{1,0:T(8,128)}, f32[24,8192]{1,0:T(8,128)S(1)}, u32[]{:S(2)}, u32[]{:S(2)}) collective-permute-start(f32[24,8192]{1,0:T(8,128)} %reshape.484), channel_id=1, source_target_pairs={{0,1},{1,2},{2,3},{3,4},{4,5},{5,6},{6,7},{7,8},{8,9},{9,10},{10,1... | collective-permute-start | bytes 2359304 | tf_op jit(solution)/shard_map/ppermute | solution.py:451
  69.8 17.5 %collective-permute-start.1 = (f32[24,8192]{1,0:T(8,128)S(1)}, f32[24,8192]{1,0:T(8,128)S(1)}, u32[]{:S(2)}, u32[]{:S(2)}) collective-permute-start(f32[24,8192]{1,0:T(8,128)S(1)} %reshape.485), channel_id=1, source_target_pairs={{1,0},{2,1},{3,2},{4,3},{5,4},{6,5},{7,6},{8,7},{9,8},{10,9},{11,1... | collective-permute-start | bytes 2359304 | tf_op jit(solution)/shard_map/ppermute | solution.py:452
  78.6 8.7 %copy-start.1 = (f32[24,8192]{1,0:T(8,128)}, f32[24,8192]{1,0:T(8,128)S(1)}, u32[]{:S(2)}) copy-start(f32[24,8192]{1,0:T(8,128)S(1)} %collective-permute-done.refs_0_.refs_1_.refs_2_) | copy-start | bytes 2359300
  87.3 0.9 copy-start.2

commit v7 on v6

--- a/solution.py
+++ b/solution.py
@@ -16,7 +16,7 @@
 
 
 DFT_PRECISION = lax.Precision.HIGH
-BLOCK = 2048
+BLOCK = 4096
 EDGE = 128
 CHUNK = 128
 ROWS = 8
@@ -102,14 +102,11 @@
 
     def chunk_body(index, carry):
         start = pl.multiple_of(index * CHUNK, CHUNK)
-        window = [
-            sums[number * ROWS : (number + 1) * ROWS, pl.ds(start, CHUNK)] * inverse_scale
-            for number in range(len(specs))
-        ]
-        powers = [window[a] + 1e-06 for a in range(dates)]
+        window = [sums[number * ROWS : (number + 1) * ROWS, pl.ds(start, CHUNK)] for number in range(len(specs))]
+        powers = [window[a] * inverse_scale + 1e-06 for a in range(dates)]
         coherence = {}
         for number, (a, b) in enumerate(pairs):
-            factor = lax.rsqrt(powers[a] * powers[b])
+            factor = lax.rsqrt(powers[a] * powers[b]) * inverse_scale
             coherence[a, b] = (
                 window[dates + 2 * number] * factor,
                 window[dates + 2 * number + 1] * factor,

time: 105 us -> 105 us (level)
  no operation moved by 1% of the time
where the time goes in v7:
time: 105 us
  waiting for transfers between devices  37.9 us (36%)
  starting transfers between devices  23.5 us (22%)
  Pallas kernels  16.3 us (16%)
  local copies, waits for them, and re-layouts  13.6 us (13%)
  other arithmetic  6.38 us (6%)
  matrix products  5.7 us (5%)
  between operations  1.25 us (1%)
    all_to_all x1, waiting for transfers between devices, shards(): tiles = lax.all_to_all(tiles, ('date', 'strip'), 0, 0, tiled=True)  22.3 us
    pallas_call x1, Pallas kernels, link_and_smooth(): pl.pallas_call(functools.partial(link_kernel, column_count, total_columns...  16.3 us
    all_to_all x1, starting transfers between devices, shards(): tiles = lax.all_to_all(tiles, ('date', 'strip'), 0, 0, tiled=True)  14.7 us
    ppermute x1, waiting for transfers between devices, shards(): lax.ppermute(image[:, :, :halo].reshape(edge_shape), axes, [(b, a) for a,...  8.7 us
    ppermute x1, waiting for transfers between devices, shards(): lax.ppermute(image[:, :, column_count - halo:].reshape(edge_shape), axes,...  6.9 us
    ppermute x1, starting transfers between devices, shards(): lax.ppermute(image[:, :, column_count - halo:].reshape(edge_shape), axes,...  6.88 us
    unnamed x31, local copies, waits for them, and re-layouts  2.68 us
    reshape x1, local copies, waits for them, and re-layouts, shards(): tiles = ranged.reshape(devices, -1, 128)  2.13 us
  transfers between devices with their start and end apart: 3, of which 3 were waited for; matrix products, arithmetic and copies ran while one was open for 5% of the time, Pallas kernels for 0%

profile of v7, /device:TPU:31, one launch (start us, length us, event | category | flops | bytes accessed | tf_op | source)
XLA Modules:
  0.0 104.7 jit_solution(9559517293827481900)
XLA Ops:
  0.6 0.1 multiply_sine_fusion.9
  0.7 0.1 fusion.55
  0.7 0.1 multiply_sine_fusion.8
  0.8 0.3 multiply_sine_fusion.1
  1.1 0.3 fusion.37
  1.3 0.3 multiply_sine_fusion
  1.6 0.3 fusion.38
  1.9 0.1 multiply_sine_fusion.7
  1.9 0.1 multiply_sine_fusion.6
  2.0 0.1 fusion.56
  2.1 1.1 %copy.47 = bf16[32,8,8,128]{3,2,1,0:T(8,128)(2,1)S(1)} copy(bf16[32,8,8,128]{3,1,2,0:T(8,128)(2,1)} %bitcast.161) | data formatting | bytes 1048576
  3.2 0.7 fusion.67
  3.9 0.1 cos.132
  4.1 0.1 sin.156
  4.2 0.5 convolution_bitcast_fusion
  4.7 0.1 multiply_subtract_fusion.5
  4.9 0.6 convolution_bitcast_fusion.7
  5.5 0.1 multiply_subtract_fusion.4
  5.7 0.6 convolution_bitcast_fusion.6
  6.3 0.1 multiply_subtract_fusion.3
  6.4 0.6 fusion.3
  7.1 1.3 %copy.14 = f32[8,128,2,2,64]{4,3,2,1,0:T(2,128)S(1)} copy(f32[8,128,2,2,64]{1,0,2,4,3:T(8,128)S(1)} %fusion.3) | data formatting | bytes 2097152 | tf_op jit(solution)/shard_map/div | solution.py:331
  8.4 2.1 %reshape.481 = f32[256,8,128]{2,1,0:T(8,128)} reshape(f32[8,128,2,2,64]{4,3,2,1,0:T(2,128)S(1)} %copy.14) | data formatting | bytes 2097152 | tf_op jit(solution)/shard_map/reshape | solution.py:430
  10.5 14.7 %all-to-all-start = ((f32[256,8,128]{2,1,0:T(8,128)}), f32[256,8,128]{2,1,0:T(8,128)S(1)}, u32[]{:S(2)}, u32[]{:S(2)}) async-start(f32[256,8,128]{2,1,0:T(8,128)} %reshape.481), calls=%async_computation | async-start | bytes 2097152 | tf_op jit(solution)/shard_map/all_to_all | solution.py:431
  25.2 0.1 fusion.66
  25.4 0.1 cos.140
  25.4 0.7 copy.18
  26.1 0.1 sin.164
  26.2 0.7 copy.19
  26.9 0.1 fusion.43
  27.1 0.1 fusion.44
  27.2 0.1 multiply_sine_fusion.5
  27.4 0.8 multiply_sine_fusion.4
  28.1 0.8 multiply_sine_fusion.3
  28.9 0.1 multiply_sine_fusion.2
  29.0 0.7 maximum_bitcast_fusion.25
  29.7 0.7 maximum_bitcast_fusion.27
  30.3 22.3 %all-to-all-done = f32[256,8,128]{2,1,0:T(8,128)S(1)} async-done(((f32[256,8,128]{2,1,0:T(8,128)}), f32[256,8,128]{2,1,0:T(8,128)S(1)}, u32[]{:S(2)}, u32[]{:S(2)}) %all-to-all-start) | async-done | bytes 1048608 | tf_op jit(solution)/shard_map/all_to_all | solution.py:431
  52.7 0.4 copy.15
  53.1 0.5 reshape.482
  53.6 0.8 copy.44
  54.4 0.3 reshape.498
  54.8 1.5 %convolution_bitcast_fusion.4 = f32[2,4,4,64,128]{4,3,0,2,1:T(8,128)S(1)} fusion(f32[2,4,4,64,128,1]{4,3,0,2,1,5:T(8,128)S(1)} %reshape.498, f32[1,2,64,64]{3,2,1,0:T(8,128)} %get-tuple-element.25, f32[1,2,64,64]{3,2,1,0:T(8,128)} %get-tuple-element.24), kind=kOutput, calls=%fused_computation.6 | convolution fusion | flops 201342976 | bytes 2162688 | tf_op jit(solution)/shard_map/pqkn,q...nm->p...km/dot_general | solution.py:292
  56.3 0.2 multiply_subtract_fusion.2
  56.5 0.6 convolution_bitcast_fusion.3
  57.2 0.2 multiply_subtract_fusion.1
  57.3 0.1 copy-done.4
  57.4 0.6 convolution_bitcast_fusion.2
  58.1 0.2 multiply_subtract_fusion
  58.2 0.0 copy-done.5
  58.3 0.0 copy-done.6
  58.3 0.6 fusion.1
  58.9 0.6 reshape.510
  59.5 0.7 copy_multiply_fusion.refs_3_.refs_4_.refs_5_
  60.2 0.5 fusion.65
  60.7 0.5 copy-done
  61.2 1.3 %reshape.484 = f32[24,8192]{1,0:T(8,128)} reshape(f32[2,4,3,8192]{3,2,1,0:T(4,128)S(1)} %get-tuple-element.15) | data formatting | bytes 1572864 | tf_op jit(solution)/shard_map/reshape | solution.py:448
  62.5 6.9 %collective-permute-start = (f32[24,8192]{1,0:T(8,128)}, f32[24,8192]{1,0:T(8,128)S(1)}, u32[]{:S(2)}, u32[]{:S(2)}) collective-permute-start(f32[24,8192]{1,0:T(8,128)} %reshape.484), channel_id=1, source_target_pairs={{0,1},{1,2},{2,3},{3,4},{4,5},{5,6},{6,7},{7,8},{8,9},{9,10},{10,1... | collective-permute-start | bytes 2359304 | tf_op jit(solution)/shard_map/ppermute | solution.py:448
  69.4 0.4 reshape.485
  69.8 1.9 %collective-permute-start.1 = (f32[24,8192]{1,0:T(8,128)S(1)}, f32[24,8192]{1,0:T(8,128)S(1)}, u32[]{:S(2)}, u32[]{:S(2)}) collective-permute-start(f32[24,8192]{1,0:T(8,128)S(1)} %reshape.485), channel_id=1, source_target_pairs={{1,0},{2,1},{3,2},{4,3},{5,4},{6,5},{7,6},{8,7},{9,8},{10,9},{11,1... | collective-permute-start | bytes 2359304 | tf_op jit(solution)/shard_map/ppermute | solution.py:449
  71.7 6.9 %collective-permute-done.refs_0_.refs_1_.refs_2_ = f32[24,8192]{1,0:T(8,128)S(1)} collective-permute-done((f32[24,8192]{1,0:T(8,128)}, f32[24,8192]{1,0:T(8,128)S(1)}, u32[]{:S(2)}, u32[]{:S(2)}) %collective-permute-start) | collective-permute-done | bytes 786464 | tf_op jit(solution)/shard_map/ppermute | solution.py:448
  78.6 8.7 %collective-permute-done.1.refs_6_.refs_7_.refs_8_ = f32[24,8192]{1,0:T(8,128)S(1)} collective-permute-done((f32[24,8192]{1,0:T(8,128)S(1)}, f32[24,8192]{1,0:T(8,128)S(1)}, u32[]{:S(2)}, u32[]{:S(2)}) %collective-permute-start.1) | collective-permute-done | bytes 786464 | tf_op jit(solution)/shard_map/ppermute | solution.py:449
  87.3 0.9 copy-done.2
  88.2 16.3 %shard_map.68 = (f32[2,4,4,8192]{3,2,1,0:T(4,128)}, f32[4,8192]{1,0:T(4,128)}) custom-call(bf16[384,128]{1,0:T(8,128)(2,1)} %constant.120.clone.band_ref, f32[24,8192]{1,0:T(8,128)} %copy-done.1, f32[24,8192]{1,0:T(8,128)} %copy-done.1, f32[24,8192]{1,0:T(8,128)} %copy-done.1, f32[2,4,4,8192]{3,2,1,0:T(4,128)} %copy-done, f32[2,4,4,8192]{3,2,1,0:T(4,128)} %copy-done, ...), custom_call_target="tpu_custom_call" | custom-call | tf_op jit(solution)/shard_map/pallas_call | solution.py:197
  (31 shorter events, 0.2 us)
Async XLA Ops:
  5.7 0.8 copy-start.3
  8.4 16.8 %copy-start.13 = (f32[8192]{0:T(1024)S(1)}, f32[8192]{0:T(1024)}, u32[]{:S(2)}) copy-start(f32[8192]{0:T(1024)} %param.7) | copy-start | bytes 98308
  10.5 42.1 %all-to-all-start = ((f32[256,8,128]{2,1,0:T(8,128)}), f32[256,8,128]{2,1,0:T(8,128)S(1)}, u32[]{:S(2)}, u32[]{:S(2)}) async-start(f32[256,8,128]{2,1,0:T(8,128)} %reshape.481), calls=%async_computation | async-start | bytes 2097152 | tf_op jit(solution)/shard_map/all_to_all | solution.py:431
  54.8 1.5 %copy-start.11 = (f32[64,128]{1,0:T(8,128)S(1)}, f32[64,128]{1,0:T(8,128)}, u32[]{:S(2)}) copy-start(f32[64,128]{1,0:T(8,128)} %get-tuple-element.46) | copy-start | bytes 98308
  54.8 1.5 %copy-start.12 = (f32[64,128]{1,0:T(8,128)S(1)}, f32[64,128]{1,0:T(8,128)}, u32[]{:S(2)}) copy-start(f32[64,128]{1,0:T(8,128)} %get-tuple-element.47) | copy-start | bytes 98308
  56.3 0.8 copy-start.7
  56.3 0.8 copy-start.8
  56.5 0.9 copy-start.4
  57.1 0.9 copy-start.9
  57.2 0.9 copy-start.10
  57.4 0.8 copy-start.5
  57.4 0.9 copy-start.6
  58.3 1.2 %copy-start.14 = (f32[4,4]{1,0:T(4,128)S(1)}, f32[4,4]{1,0:T(4,128)}, u32[]{:S(2)}) copy-start(f32[4,4]{1,0:T(4,128)} %param.8) | copy-start | bytes 196
  60.2 1.0 copy-start
  62.5 16.1 %collective-permute-start = (f32[24,8192]{1,0:T(8,128)}, f32[24,8192]{1,0:T(8,128)S(1)}, u32[]{:S(2)}, u32[]{:S(2)}) collective-permute-start(f32[24,8192]{1,0:T(8,128)} %reshape.484), channel_id=1, source_target_pairs={{0,1},{1,2},{2,3},{3,4},{4,5},{5,6},{6,7},{7,8},{8,9},{9,10},{10,1... | collective-permute-start | bytes 2359304 | tf_op jit(solution)/shard_map/ppermute | solution.py:448
  69.8 17.5 %collective-permute-start.1 = (f32[24,8192]{1,0:T(8,128)S(1)}, f32[24,8192]{1,0:T(8,128)S(1)}, u32[]{:S(2)}, u32[]{:S(2)}) collective-permute-start(f32[24,8192]{1,0:T(8,128)S(1)} %reshape.485), channel_id=1, source_target_pairs={{1,0},{2,1},{3,2},{4,3},{5,4},{6,5},{7,6},{8,7},{9,8},{10,9},{11,1... | collective-permute-start | bytes 2359304 | tf_op jit(solution)/shard_map/ppermute | solution.py:449
  78.6 8.7 %copy-start.1 = (f32[24,8192]{1,0:T(8,128)}, f32[24,8192]{1,0:T(8,128)S(1)}, u32[]{:S(2)}) copy-start(f32[24,8192]{1,0:T(8,128)S(1)} %collective-permute-done.refs_0_.refs_1_.refs_2_) | copy-start | bytes 2359300
  87.3 0.9 copy-start.2
